TPU v7x, 128 devices: a whole 4x4x4 slice. The times are simulated.
128 devices in a mesh: seq: 4 (over x_hi, core), tensor: 32 (over y, x_lo, z).
Axes of the slice: x: 4 (x_hi: 2, x_lo: 2; x = x_hi * 2 + x_lo), y: 4, z: 4, core: 2. Of those that a mesh axis runs over, the one named last changes fastest.
Arguments:
- hidden_in: bfloat16 [8192, 4608], P(('seq', 'tensor'))
- norm_gain: float32 [4608], replicated, may hold values from 0.5 to 1.5
- query_weight: bfloat16 [4608, 4096], P(None, 'tensor')
- key_weight: bfloat16 [4608, 2048], P(None, 'tensor'), may hold values from -0.09375 to 0.09375
- value_weight: bfloat16 [4608, 2048], P(None, 'tensor'), may hold values from -0.09375 to 0.09375
- out_weight: bfloat16 [4096, 4608], P('tensor'), may hold values from -0.09375 to 0.09375
- post_gain: float32 [4608], replicated, may hold values from 0.5 to 1.5
- seg_lengths: int32 [3], replicated, may hold values from 256 to 4096, as said below
- segment_ids: int32 [8192], replicated, may hold values from 0 to 2, as said below
- slot_map: int32 [3], replicated, may hold values from 0 to 2, each once
Outputs:
- hidden_out: bfloat16 [8192, 4608], P(('seq', 'tensor'))
- key_cache: bfloat16 [3, 4096, 2048], P(None, 'seq', 'tensor')
- value_cache: bfloat16 [3, 4096, 2048], P(None, 'seq', 'tensor')
Inputs may be any that keep to these rules, and one draw needn't show every extreme that they name: `seg_lengths`: the 3 lengths sum to 8192; the second request is the longest, with exactly 4096 tokens. `segment_ids`: requests follow one another in order: request r holds seg_lengths[r] consecutive tokens, starting where request r - 1 ends. `slot_map`: each cache slot is named by exactly one request.
All inputs are finite; a program needn't handle non-finite values.
Results may differ from a plain program's by a relative error of at most 0.02.
Values may be sent and summed in bfloat16 or wider, within the bound.
No kernel may reach another device: no remote copies, remote signals or barrier semaphores. Data moves between devices by JAX's collectives and lax.ppermute only.
A program may use at most 128 MiB of HBM per device.

v0:
```python
import jax
import jax.numpy as jnp
import numpy as np
from jax import lax
from jax.sharding import Mesh
from jax.sharding import PartitionSpec as P

HD = 128


EPSILON = 1e-06
SOFTCAP = 50.0
QUERY_SCALE = 144.0 ** (-0.5)
SCORE_SHIFT = 20.0
ROPE_BASE = 10000.0
KEY_TILE = 512
Q_CHUNKS = 2
HEADS_PER_DEVICE = 4


def rms_scale(values, gain):
    mean_sq = jnp.mean(values * values, axis=-1, keepdims=True)
    return values * lax.rsqrt(mean_sq + EPSILON) * gain


def rotate(values, positions):
    head_dim = values.shape[-1]
    half_dim = head_dim // 2
    freqs = ROPE_BASE ** (-2.0 * jnp.arange(half_dim, dtype=jnp.float32) / head_dim)
    angles = positions.astype(jnp.float32)[:, None] * freqs[None, :]
    cosine = jnp.cos(angles)[:, None, :]
    sine = jnp.sin(angles)[:, None, :]
    first = values[..., :half_dim]
    second = values[..., half_dim:]
    return jnp.concatenate(
        [first * cosine - second * sine, second * cosine + first * sine], axis=-1
    )


def segment_starts_of(row_segments, seg_lengths):
    starts = jnp.cumsum(seg_lengths) - seg_lengths
    request_ids = jnp.arange(seg_lengths.shape[0], dtype=jnp.int32)
    return jnp.sum(
        jnp.where(row_segments[:, None] == request_ids[None, :], starts[None, :], 0), axis=1
    )


def on_device(
    hidden_in,
    norm_gain,
    query_weight,
    key_weight,
    value_weight,
    out_weight,
    post_gain,
    seg_lengths,
    segment_ids,
    slot_map,
):
    n_group = lax.axis_size("th")
    n_seq = lax.axis_size("seq")
    n_pair = lax.axis_size("tl")
    kv_local = n_pair // 2
    local_rows = hidden_in.shape[0]
    tokens = segment_ids.shape[0]
    group_rows = local_rows * n_group
    seq_rows = group_rows * n_pair
    head_dim = HD
    half_kv = key_weight.shape[1]
    seq_index = lax.axis_index("seq")
    pair_index = lax.axis_index("tl")
    slot_count = seg_lengths.shape[0]

    hidden = hidden_in.astype(jnp.float32)
    normed = rms_scale(hidden, norm_gain).astype(jnp.bfloat16)

    own_joined = jnp.concatenate([query_weight, key_weight, value_weight], axis=1)
    core = seq_index % 2
    fetched = lax.all_gather(
        jnp.where(core == 0, query_weight, jnp.concatenate([key_weight, value_weight], 1)),
        "tl",
        axis=0,
        tiled=False,
    )
    swapped = lax.ppermute(fetched, "seq", [(i, i ^ 1) for i in range(n_seq)])
    pair_out = lax.all_gather(out_weight, "tl", axis=0, tiled=True)

    spread = jnp.broadcast_to(normed[None], (n_group,) + normed.shape)
    gathered = lax.all_to_all(spread, "th", 0, 0, tiled=True).reshape(group_rows, -1)
    width = own_joined.shape[1]
    mixed_fetched = jnp.einsum(
        "rd,cdw->rcw", gathered, fetched, preferred_element_type=jnp.float32
    )
    mixed_swapped = jnp.einsum(
        "rd,cdw->rcw", gathered, swapped, preferred_element_type=jnp.float32
    )
    mixed = jnp.where(
        core == 0,
        jnp.concatenate([mixed_fetched, mixed_swapped], 2),
        jnp.concatenate([mixed_swapped, mixed_fetched], 2),
    )
    queries = mixed[:, :, :head_dim]
    full_key = mixed[:, :, head_dim : head_dim + half_kv].reshape(
        group_rows, kv_local, 2 * half_kv
    )
    full_value = mixed[:, :, head_dim + half_kv :].reshape(group_rows, kv_local, 2 * half_kv)

    member = jnp.arange(group_rows, dtype=jnp.int32) // local_rows
    within = jnp.arange(group_rows, dtype=jnp.int32) % local_rows
    row_ids = seq_index * seq_rows + (member * n_pair + pair_index) * local_rows + within
    row_segments = jnp.take(segment_ids, row_ids)
    positions = row_ids - segment_starts_of(row_segments, seg_lengths)

    q_rot = rotate(queries, positions).astype(jnp.bfloat16)
    k_rot = rotate(full_key, positions).astype(jnp.bfloat16)
    v_bf = full_value.astype(jnp.bfloat16)

    kv = jnp.stack([jnp.transpose(k_rot, (1, 0, 2)), jnp.transpose(v_bf, (1, 0, 2))])
    kv_all = lax.all_gather(kv, ("seq", "tl"), axis=2, tiled=True)
    kv_all = kv_all.reshape(2, kv_local, n_seq, n_pair, n_group, local_rows, head_dim)
    kv_all = jnp.transpose(kv_all, (0, 1, 2, 4, 3, 5, 6)).reshape(2, kv_local, tokens, head_dim)
    key_rows = kv_all[0]
    value_rows = kv_all[1]

    chunk_rows = group_rows // Q_CHUNKS
    member_part = local_rows // Q_CHUNKS
    q_chunks = jnp.transpose(
        q_rot.reshape(n_group, Q_CHUNKS, member_part, n_pair, head_dim), (1, 0, 2, 3, 4)
    ).reshape(Q_CHUNKS, chunk_rows, kv_local, 2, head_dim)
    q_ids = jnp.transpose(row_ids.reshape(n_group, Q_CHUNKS, member_part), (1, 0, 2)).reshape(
        Q_CHUNKS, chunk_rows
    )
    q_segs = jnp.transpose(
        row_segments.reshape(n_group, Q_CHUNKS, member_part), (1, 0, 2)
    ).reshape(Q_CHUNKS, chunk_rows)
    q_pos = jnp.transpose(positions.reshape(n_group, Q_CHUNKS, member_part), (1, 0, 2)).reshape(
        Q_CHUNKS, chunk_rows
    )

    def attend(chunk):
        def tile(tile_index, state):
            numer_one, denom_one = state
            k_start = tile_index * KEY_TILE
            k_block = lax.dynamic_slice_in_dim(key_rows, k_start, KEY_TILE, 1)
            v_block = lax.dynamic_slice_in_dim(value_rows, k_start, KEY_TILE, 1)
            k_segs = lax.dynamic_slice_in_dim(segment_ids, k_start, KEY_TILE, 0)
            k_ids = k_start + jnp.arange(KEY_TILE, dtype=jnp.int32)

            scores = (
                jnp.einsum(
                    "qkgd,ktd->kgqt",
                    q_chunks[chunk],
                    k_block,
                    preferred_element_type=jnp.float32,
                )
                * QUERY_SCALE
            )
            scores = SOFTCAP * jnp.tanh(scores / SOFTCAP)
            live = (k_ids[None, :] <= q_ids[chunk][:, None]) & (
                k_segs[None, :] == q_segs[chunk][:, None]
            )
            weights = jnp.where(live[None, None], jnp.exp(scores - SCORE_SHIFT), 0.0)
            denom_one = denom_one + jnp.sum(weights, axis=-1)
            numer_one = numer_one + jnp.einsum(
                "kgqt,ktd->qkgd",
                weights.astype(jnp.bfloat16),
                v_block,
                preferred_element_type=jnp.float32,
            )
            return (numer_one, denom_one)

        zero_numer = jnp.zeros((chunk_rows, kv_local, 2, head_dim), jnp.float32)
        zero_denom = jnp.zeros((kv_local, 2, chunk_rows), jnp.float32)
        lo_tile = jnp.min(q_ids[chunk] - q_pos[chunk]) // KEY_TILE
        hi_tile = jnp.max(q_ids[chunk]) // KEY_TILE + 1
        numer, denom = lax.fori_loop(lo_tile, hi_tile, tile, (zero_numer, zero_denom))
        denom_rows = jnp.transpose(denom, (2, 0, 1))[..., None]
        attended = (numer / denom_rows).astype(jnp.bfloat16).reshape(
            chunk_rows, n_pair * head_dim
        )
        partial = jnp.dot(attended, pair_out, preferred_element_type=jnp.float32).astype(
            jnp.bfloat16
        )
        pieces = lax.all_to_all(
            partial.reshape(n_group, member_part, -1), "th", 0, 0, tiled=True
        )
        return jnp.sum(pieces.astype(jnp.float32), axis=0)

    projected = jnp.concatenate([attend(chunk) for chunk in range(Q_CHUNKS)], axis=0)
    hidden_out = (hidden + rms_scale(projected, post_gain)).astype(jnp.bfloat16)

    cache_len = tokens // 2
    part_len = cache_len // n_seq
    request_ids = jnp.arange(slot_count, dtype=jnp.int32)
    starts = jnp.cumsum(seg_lengths) - seg_lengths
    own_head = pair_index // 2
    own_offset = pair_index % 2 * half_kv
    own_keys = lax.dynamic_slice_in_dim(
        lax.dynamic_index_in_dim(key_rows, own_head, 0, keepdims=False), own_offset, half_kv, 1
    )
    own_values = lax.dynamic_slice_in_dim(
        lax.dynamic_index_in_dim(value_rows, own_head, 0, keepdims=False), own_offset, half_kv, 1
    )
    keys_pad = jnp.concatenate([own_keys, jnp.zeros((cache_len, half_kv), jnp.bfloat16)], 0)
    values_pad = jnp.concatenate(
        [own_values, jnp.zeros((cache_len, half_kv), jnp.bfloat16)], 0
    )
    seg_pad = jnp.concatenate([segment_ids, jnp.full((cache_len,), -1, jnp.int32)], 0)
    key_slots = []
    value_slots = []
    for slot_index in range(slot_count):
        request = jnp.sum(jnp.where(slot_map == slot_index, request_ids, 0)).astype(jnp.int32)
        first_row = jnp.sum(jnp.where(request_ids == request, starts, 0)).astype(jnp.int32)
        row0 = first_row + seq_index * part_len
        keep = (lax.dynamic_slice_in_dim(seg_pad, row0, part_len, 0) == request)[:, None]
        key_slots.append(
            jnp.where(
                keep,
                lax.dynamic_slice_in_dim(keys_pad, row0, part_len, 0),
                jnp.zeros((), jnp.bfloat16),
            )
        )
        value_slots.append(
            jnp.where(
                keep,
                lax.dynamic_slice_in_dim(values_pad, row0, part_len, 0),
                jnp.zeros((), jnp.bfloat16),
            )
        )
    return (hidden_out, jnp.stack(key_slots), jnp.stack(value_slots))


def solution(mesh):
    devices = np.asarray(mesh.devices)
    n_seq, n_tensor = devices.shape
    split = Mesh(
        devices.reshape(n_seq, n_tensor // HEADS_PER_DEVICE, HEADS_PER_DEVICE),
        ("seq", "th", "tl"),
    )
    rows = P(("seq", "th", "tl"), None)
    cols = P(None, ("th", "tl"))
    return jax.shard_map(
        on_device,
        mesh=split,
        in_specs=(
            rows,
            P(),
            cols,
            cols,
            cols,
            P(("th", "tl"), None),
            P(),
            P(),
            P(),
            P(),
        ),
        out_specs=(rows, P(None, "seq", ("th", "tl")), P(None, "seq", ("th", "tl"))),
        check_vma=False,
    )
```

profile of v0, /device:TPU:7, one launch (start us, length us, event | category | flops | bytes accessed | tf_op | source)
XLA Modules:
  0.0 312.4 jit_solution(6902794422364136423)
XLA Ops:
  12.0 2.6 broadcast_in_dim.133
  14.5 5.4 %all-to-all-start = ((bf16[8,64,4608]{2,1,0:T(8,128)(2,1)}), bf16[8,64,4608]{2,1,0:T(8,128)(2,1)}, u32[]{:S(2)}, u32[]{:S(2)}) async-start(bf16[8,64,4608]{2,1,0:T(8,128)(2,1)} %broadcast_in_dim.133), calls=%async_computation | async-start | bytes 9437184 | tf_op jit(solution)/shard_map/all_to_all | solution.py:89
  19.9 48.0 %all-gather.9.cloned.1.call-done = bf16[18432,128]{1,0:T(8,128)(2,1)} async-done(((bf16[4608,128]{1,0:T(8,128)(2,1)}), bf16[18432,128]{1,0:T(8,128)(2,1)}) %all-gather.9.cloned.1.call-update) | async-done | bytes 4718608 | tf_op jit(solution)/shard_map/all_gather | solution.py:79
  67.9 6.8 %copy.82 = bf16[4,4608,128]{1,2,0:T(8,128)(2,1)} copy(bf16[4,4608,128]{2,1,0:T(8,128)(2,1)} %bitcast.153) | data formatting | bytes 9437184 | tf_op jit(solution)/shard_map/all_gather | solution.py:79
  75.8 3.1 %gather_fusion = s32[512]{0:T(512)S(1)} fusion(s32[8192]{0:T(1024)S(1)} %copy-done, s32[1024]{0:T(1024)S(1)} %pad_clamp_fusion), kind=kCustom, calls=%fused_computation | custom fusion | bytes 6144 | tf_op jit(solution)/shard_map/jit(_take)/gather | solution.py:111
  79.6 2.6 fusion.51
  83.1 5.9 %fusion.60 = f32[512,512]{0,1:S(1)} fusion(bf16[512,4608]{1,0:T(8,128)(2,1)} %bitcast.22, bf16[4608,512]{0,1:T(8,128)(2,1)} %bitcast.152), kind=kOutput, calls=%fused_computation.160 | convolution fusion | flops 2415919104 | bytes 10485760
  89.1 5.9 %fusion.61 = f32[512,512]{0,1:S(1)} fusion(bf16[512,4608]{1,0:T(8,128)(2,1)} %bitcast.22, bf16[4608,512]{0,1:T(8,128)(2,1)} %bitcast.28), kind=kOutput, calls=%fused_computation.161 | convolution fusion | flops 2415919104 | bytes 10485760
  110.1 59.0 %all-gather.5.cloned.1.call-done = bf16[2,2,8192,128]{3,2,1,0:T(8,128)(2,1)} async-done(((bf16[2,2,512,128]{3,2,1,0:T(8,128)(2,1)}), bf16[2,2,8192,128]{3,2,1,0:T(8,128)(2,1)}) %all-gather.5.cloned.1.call-update) | async-done | bytes 8388624 | tf_op jit(solution)/shard_map/all_gather | solution.py:119
  169.0 4.4 %fusion.58 = (bf16[1,2,4,8,4,64,128]{6,5,3,4,2,1,0:T(8,128)(2,1)S(1)}, bf16[1,2,4,8,4,64,128]{6,5,3,4,2,1,0:T(8,128)(2,1)S(1)}) fusion(bf16[2,2,4,8,4,64,128]{6,5,3,4,2,1,0:T(8,128)(2,1)} %bitcast.151), kind=kLoop, calls=%fused_computation.158 | loop fusion | bytes 16777216 | tf_op jit(solution)/shard_map/slice | solution.py:122
  173.5 2.9 copy.89
  176.4 2.9 copy.91
  179.3 6.5 %copy.95 = bf16[2,8192,128]{1,2,0:T(8,128)(2,1)} copy(bf16[2,8192,128]{2,1,0:T(8,128)(2,1)} %bitcast.146) | data formatting | bytes 8388608 | tf_op jit(solution)/shard_map/while | solution.py:176
  185.9 37.9 %while.28 = (s32[]{:T(128)}, f32[256,2,2,128]{0,3,2,1:T(8,128)S(1)}, f32[2,2,256]{2,1,0:T(2,128)S(1)}, s32[]{:T(128)}, bf16[2,8192,128]{1,2,0:T(8,128)(2,1)}, /*...) while((s32[]{:T(128)}, ...), condition=%wide.region_7.8_spmd, body=%wide.region_5.7_spmd.sunk | while | flops 272105984 | bytes 4227267 | solution.py:176
  223.9 5.3 %convolution_convert_fusion.1 = bf16[256,4608]{1,0:T(8,128)(2,1)} fusion(bf16[256,512]{0,1:T(8,128)(2,1)S(1)} %bitcast.159, bf16[512,4608]{1,0:T(8,128)(2,1)} %all-gather.7.cloned.1.call-done), kind=kOutput, calls=%fused_computation.30 | convolution fusion | flops 1209139200 | bytes 7340032 | tf_op jit(solution)/shard_map/dot_general | solution.py:181
  229.2 5.2 %all-to-all-start.1 = ((bf16[8,32,4608]{2,1,0:T(8,128)(2,1)}), bf16[8,32,4608]{2,1,0:T(8,128)(2,1)S(1)}, u32[]{:S(2)}, u32[]{:S(2)}) async-start(bf16[8,32,4608]{2,1,0:T(8,128)(2,1)} %bitcast.150), calls=%async_computation.1 | async-start | bytes 4718592 | tf_op jit(solution)/shard_map/all_to_all | solution.py:184
  234.4 38.8 %while.29 = (s32[]{:T(128)}, f32[256,2,2,128]{0,3,2,1:T(8,128)S(1)}, f32[2,2,256]{2,1,0:T(2,128)S(1)}, s32[]{:T(128)}, bf16[2,8192,128]{1,2,0:T(8,128)(2,1)}, /*...) while((s32[]{:T(128)}, ...), condition=%wide.region_13.14_spmd, body=%wide.region_11.13_spmd.sunk | while | flops 272105984 | bytes 4227267 | solution.py:176
  273.3 5.1 %convolution_convert_fusion = bf16[256,4608]{1,0:T(8,128)(2,1)} fusion(bf16[256,512]{0,1:T(8,128)(2,1)S(1)} %bitcast.160, bf16[512,4608]{1,0:T(8,128)(2,1)} %all-gather.7.cloned.1.call-done), kind=kOutput, calls=%fused_computation.29 | convolution fusion | flops 1209139200 | bytes 7340032 | tf_op jit(solution)/shard_map/dot_general | solution.py:181
  278.4 5.1 %all-to-all-start.2 = ((bf16[8,32,4608]{2,1,0:T(8,128)(2,1)}), bf16[8,32,4608]{2,1,0:T(8,128)(2,1)}, u32[]{:S(2)}, u32[]{:S(2)}) async-start(bf16[8,32,4608]{2,1,0:T(8,128)(2,1)} %bitcast.149), calls=%async_computation.2 | async-start | bytes 4718592 | tf_op jit(solution)/shard_map/all_to_all | solution.py:184
  285.6 1.9 fusion.31
  287.5 5.3 %constant_dynamic-slice_fusion = (bf16[1,8192,64]{2,1,0:T(8,128)(2,1)}, bf16[1,8192,64]{2,1,0:T(8,128)(2,1)}) fusion(bf16[2,8192,128]{2,1,0:T(8,128)(2,1)} %bitcast.147, s32[]{:T(128)S(6)} %select_n.271, s32[]{:T(128)S(6)} %select_n.274, bf16[2,8192,128]{2,1,0:T(8,128)(2,1)} %get-tuple-element.661), kind=kLoop, calls=%fused_computation.135 | loop fusion | bytes 4194312 | tf_op jit(solution)/shard_map/dynamic_slice | solution.py:201
  292.8 2.7 copy.97
  295.5 2.7 copy.98
  302.5 2.1 convert_reduce_fusion
  (262 shorter events, 93.9 us)
Async XLA Ops:
  7.2 1.8 copy-start.3
  7.2 60.8 %all-gather.9.cloned.1.call-start = ((), (), s32[]{:S(2)}) async-start(), calls=%async_computation.5 | async-start | bytes 5898240 | tf_op jit(solution)/shard_map/all_gather | solution.py:79
  9.7 1.9 copy-start.1
  9.7 2.1 copy-start.5
  14.5 68.6 %all-to-all-start = ((bf16[8,64,4608]{2,1,0:T(8,128)(2,1)}), bf16[8,64,4608]{2,1,0:T(8,128)(2,1)}, u32[]{:S(2)}, u32[]{:S(2)}) async-start(bf16[8,64,4608]{2,1,0:T(8,128)(2,1)} %broadcast_in_dim.133), calls=%async_computation | async-start | bytes 9437184 | tf_op jit(solution)/shard_map/all_to_all | solution.py:89
  19.9 149.1 %all-gather.5.cloned.1.call-start = ((), (), s32[]{:S(2)}) async-start(), calls=%async_computation.3 | async-start | bytes 8912896 | tf_op jit(solution)/shard_map/all_gather | solution.py:119
  67.9 7.6 %copy-start.7 = (s32[3]{0:T(128)S(1)}, s32[3]{0:T(128)}, u32[]{:S(2)}) copy-start(s32[3]{0:T(128)} %param.21) | copy-start | bytes 40
  67.9 7.8 %copy-start = (s32[8192]{0:T(1024)S(1)}, s32[8192]{0:T(1024)}, u32[]{:S(2)}) copy-start(s32[8192]{0:T(1024)} %param.22) | copy-start | bytes 98308
  74.7 4.2 %copy-start.8 = (s32[3]{0:T(128)S(1)}, s32[3]{0:T(128)}, u32[]{:S(2)}) copy-start(s32[3]{0:T(128)} %param.23) | copy-start | bytes 40
  74.7 14.3 %collective-permute-start = (bf16[4,4608,128]{1,2,0:T(8,128)(2,1)}, bf16[4,4608,128]{1,2,0:T(8,128)(2,1)}, u32[]{:S(2)}, u32[]{:S(2)}) collective-permute-start(bf16[4,4608,128]{1,2,0:T(8,128)(2,1)} %copy.82), channel_id=1, source_target_pairs={{0,32},{32,0},{64,96},{96,64},{1,33},{33,1},{65,97},{97,65},{2,34}... | collective-permute-start | bytes 14155784 | tf_op jit(solution)/shard_map/ppermute | solution.py:85
  97.4 126.5 %all-gather.7.cloned.1.call-start = ((), (), s32[]{:S(2)}) async-start(), calls=%async_computation.4 | async-start | bytes 5898240 | tf_op jit(solution)/shard_map/all_gather | solution.py:86
  223.8 5.4 %copy-start.4 = (bf16[2,256,2,2,128]{4,1,3,2,0:T(8,128)(2,1)}, bf16[2,256,2,2,128]{4,1,3,2,0:T(8,128)(2,1)S(1)}, u32[]{:S(2)}) copy-start(bf16[2,256,2,2,128]{4,1,3,2,0:T(8,128)(2,1)S(1)} %get-tuple-element.676) | copy-start | bytes 1572868
  229.2 49.3 %all-to-all-start.1 = ((bf16[8,32,4608]{2,1,0:T(8,128)(2,1)}), bf16[8,32,4608]{2,1,0:T(8,128)(2,1)S(1)}, u32[]{:S(2)}, u32[]{:S(2)}) async-start(bf16[8,32,4608]{2,1,0:T(8,128)(2,1)} %bitcast.150), calls=%async_computation.1 | async-start | bytes 4718592 | tf_op jit(solution)/shard_map/all_to_all | solution.py:184
  278.4 24.1 %all-to-all-start.2 = ((bf16[8,32,4608]{2,1,0:T(8,128)(2,1)}), bf16[8,32,4608]{2,1,0:T(8,128)(2,1)}, u32[]{:S(2)}, u32[]{:S(2)}) async-start(bf16[8,32,4608]{2,1,0:T(8,128)(2,1)} %bitcast.149), calls=%async_computation.2 | async-start | bytes 4718592 | tf_op jit(solution)/shard_map/all_to_all | solution.py:184
  302.5 2.1 copy-start.2
  302.5 2.3 copy-start.6
Sparse Core Ops, SparseCore 0:
  11.7 56.2 all-gather.8
  97.5 71.4 all-gather.4
  170.7 51.4 all-gather.6
where the time goes:
time: 313 us; the launch traced here: 312 us
  waiting for transfers between devices  108 us (35%)
  matrix products  91.2 us (29%)
  local copies, waits for them, and re-layouts  46.3 us (15%)
  between operations  25.8 us (8%)
  other arithmetic  23.6 us (8%)
  starting transfers between devices  16.8 us (5%)
    all_gather x1, waiting for transfers between devices, on_device(): kv_all = lax.all_gather(kv, ('seq', 'tl'), axis=2, tiled=True)  59 us
    all_gather x1, waiting for transfers between devices, on_device(): lax.all_gather(jnp.where(core == 0, query_weight, jnp.concatenate([key_we...  48 us
    dot_general x22, matrix products, tile(): jnp.einsum('qkgd,ktd->kgqt', q_chunks[chunk], k_block, preferred_element_...  40.9 us
    dot_general x22, matrix products, tile(): jnp.einsum('kgqt,ktd->qkgd', weights.astype(jnp.bfloat16), v_block, prefe...  28.1 us
    unnamed x2, matrix products  11.8 us
    dot_general x2, matrix products, attend(): jnp.dot(attended, pair_out, preferred_element_type=jnp.float32)  10.4 us
    all_to_all x2, starting transfers between devices, attend(): lax.all_to_all(partial.reshape(n_group, member_part, -1), 'th', 0, 0, til...  10.3 us
    dynamic_slice x2, local copies, waits for them, and re-layouts, on_device(): lax.dynamic_slice_in_dim(lax.dynamic_index_in_dim(value_rows, own_head, 0...  8.05 us
  transfers between devices with their start and end apart: 7, of which 2 were waited for; matrix products, arithmetic and copies ran while one was open for 45% of the time, Pallas kernels for 0%

commit v1 on v0

--- a/solution.py
+++ b/solution.py
@@ -58,7 +58,7 @@
     slot_map,
 ):
     n_group = lax.axis_size("th")
-    n_seq = lax.axis_size("seq")
+    n_seq = lax.axis_size("sh") * lax.axis_size("core")
     n_pair = lax.axis_size("tl")
     kv_local = n_pair // 2
     local_rows = hidden_in.shape[0]
@@ -67,7 +67,8 @@
     seq_rows = group_rows * n_pair
     head_dim = HD
     half_kv = key_weight.shape[1]
-    seq_index = lax.axis_index("seq")
+    core = lax.axis_index("core")
+    seq_index = lax.axis_index("sh") * lax.axis_size("core") + core
     pair_index = lax.axis_index("tl")
     slot_count = seg_lengths.shape[0]
 
@@ -75,14 +76,13 @@
     normed = rms_scale(hidden, norm_gain).astype(jnp.bfloat16)
 
     own_joined = jnp.concatenate([query_weight, key_weight, value_weight], axis=1)
-    core = seq_index % 2
     fetched = lax.all_gather(
         jnp.where(core == 0, query_weight, jnp.concatenate([key_weight, value_weight], 1)),
         "tl",
         axis=0,
         tiled=False,
     )
-    swapped = lax.ppermute(fetched, "seq", [(i, i ^ 1) for i in range(n_seq)])
+    swapped = lax.ppermute(fetched, "core", [(0, 1), (1, 0)])
     pair_out = lax.all_gather(out_weight, "tl", axis=0, tiled=True)
 
     spread = jnp.broadcast_to(normed[None], (n_group,) + normed.shape)
@@ -116,9 +116,19 @@
     v_bf = full_value.astype(jnp.bfloat16)
 
     kv = jnp.stack([jnp.transpose(k_rot, (1, 0, 2)), jnp.transpose(v_bf, (1, 0, 2))])
-    kv_all = lax.all_gather(kv, ("seq", "tl"), axis=2, tiled=True)
-    kv_all = kv_all.reshape(2, kv_local, n_seq, n_pair, n_group, local_rows, head_dim)
-    kv_all = jnp.transpose(kv_all, (0, 1, 2, 4, 3, 5, 6)).reshape(2, kv_local, tokens, head_dim)
+    mine = lax.all_gather(kv, ("sh", "tl"), axis=2, tiled=True)
+    theirs = lax.ppermute(mine, "core", [(0, 1), (1, 0)])
+    n_sh = n_seq // 2
+    mine = mine.reshape(2, kv_local, n_sh, 1, n_pair, n_group, local_rows, head_dim)
+    theirs = theirs.reshape(2, kv_local, n_sh, 1, n_pair, n_group, local_rows, head_dim)
+    kv_all = jnp.where(
+        core == 0,
+        jnp.concatenate([mine, theirs], axis=3),
+        jnp.concatenate([theirs, mine], axis=3),
+    )
+    kv_all = jnp.transpose(kv_all, (0, 1, 2, 3, 5, 4, 6, 7)).reshape(
+        2, kv_local, tokens, head_dim
+    )
     key_rows = kv_all[0]
     value_rows = kv_all[1]
 
@@ -234,10 +244,10 @@
     devices = np.asarray(mesh.devices)
     n_seq, n_tensor = devices.shape
     split = Mesh(
-        devices.reshape(n_seq, n_tensor // HEADS_PER_DEVICE, HEADS_PER_DEVICE),
-        ("seq", "th", "tl"),
-    )
-    rows = P(("seq", "th", "tl"), None)
+        devices.reshape(n_seq // 2, 2, n_tensor // HEADS_PER_DEVICE, HEADS_PER_DEVICE),
+        ("sh", "core", "th", "tl"),
+    )
+    rows = P(("sh", "core", "th", "tl"), None)
     cols = P(None, ("th", "tl"))
     return jax.shard_map(
         on_device,
@@ -254,6 +264,10 @@
             P(),
             P(),
         ),
-        out_specs=(rows, P(None, "seq", ("th", "tl")), P(None, "seq", ("th", "tl"))),
+        out_specs=(
+            rows,
+            P(None, ("sh", "core"), ("th", "tl")),
+            P(None, ("sh", "core"), ("th", "tl")),
+        ),
         check_vma=False,
     )

time: 313 us -> 333 us (1.064)
  the two profiles are of different devices: /device:TPU:7 before, /device:TPU:4 now
where the time goes in v1:
time: 333 us; the launch traced here: 337 us
  waiting for transfers between devices  117 us (35%)
  matrix products  97.5 us (29%)
  local copies, waits for them, and re-layouts  45.2 us (14%)
  other arithmetic  33.9 us (10%)
  between operations  25.9 us (8%)
  starting transfers between devices  16.7 us (5%)
    all_gather x1, waiting for transfers between devices, on_device(): mine = lax.all_gather(kv, ('sh', 'tl'), axis=2, tiled=True)  69.3 us
    all_gather x1, waiting for transfers between devices, on_device(): lax.all_gather(jnp.where(core == 0, query_weight, jnp.concatenate([key_we...  47.1 us
    dot_general x24, matrix products, tile(): jnp.einsum('qkgd,ktd->kgqt', q_chunks[chunk], k_block, preferred_element_...  44.6 us
    dot_general x24, matrix products, tile(): jnp.einsum('kgqt,ktd->qkgd', weights.astype(jnp.bfloat16), v_block, prefe...  30.6 us
    unnamed x2, matrix products  11.8 us
    all_to_all x2, starting transfers between devices, attend(): lax.all_to_all(partial.reshape(n_group, member_part, -1), 'th', 0, 0, til...  11.5 us
    dot_general x2, matrix products, attend(): jnp.dot(attended, pair_out, preferred_element_type=jnp.float32)  10.4 us
    transpose x1, other arithmetic, on_device(): jnp.transpose(kv_all, (0, 1, 2, 3, 5, 4, 6, 7))  8.42 us
  transfers between devices with their start and end apart: 8, of which 2 were waited for; matrix products, arithmetic and copies ran while one was open for 46% of the time, Pallas kernels for 0%

profile of v1, /device:TPU:4, one launch (start us, length us, event | category | flops | bytes accessed | tf_op | source)
XLA Modules:
  0.0 337.0 jit_solution(11400934871926197648)
XLA Ops:
  9.7 3.1 maximum_select_fusion.2
  13.3 2.6 broadcast_in_dim.133
  15.9 5.1 %all-to-all-start = ((bf16[8,64,4608]{2,1,0:T(8,128)(2,1)}), bf16[8,64,4608]{2,1,0:T(8,128)(2,1)}, u32[]{:S(2)}, u32[]{:S(2)}) async-start(bf16[8,64,4608]{2,1,0:T(8,128)(2,1)} %broadcast_in_dim.133), calls=%async_computation | async-start | bytes 9437184 | tf_op jit(solution)/shard_map/all_to_all | solution.py:89
  21.0 47.1 %all-gather.9.cloned.1.call-done = bf16[18432,128]{1,0:T(8,128)(2,1)} async-done(((bf16[4608,128]{1,0:T(8,128)(2,1)}), bf16[18432,128]{1,0:T(8,128)(2,1)}) %all-gather.9.cloned.1.call-update) | async-done | bytes 4718608 | tf_op jit(solution)/shard_map/all_gather | solution.py:79
  68.1 6.8 %copy.85 = bf16[4,4608,128]{1,2,0:T(8,128)(2,1)} copy(bf16[4,4608,128]{2,1,0:T(8,128)(2,1)} %bitcast.153) | data formatting | bytes 9437184 | tf_op jit(solution)/shard_map/all_gather | solution.py:79
  75.1 3.1 gather_fusion
  79.0 2.6 fusion.52
  82.5 5.9 %fusion.61 = f32[512,512]{0,1:S(1)} fusion(bf16[512,4608]{1,0:T(8,128)(2,1)} %bitcast.22, bf16[4608,512]{0,1:T(8,128)(2,1)} %bitcast.152), kind=kOutput, calls=%fused_computation.162 | convolution fusion | flops 2415919104 | bytes 10485760
  88.4 5.9 %fusion.62 = f32[512,512]{0,1:S(1)} fusion(bf16[512,4608]{1,0:T(8,128)(2,1)} %bitcast.22, bf16[4608,512]{0,1:T(8,128)(2,1)} %bitcast.28), kind=kOutput, calls=%fused_computation.163 | convolution fusion | flops 2415919104 | bytes 10485760
  96.8 69.3 %all-gather.5.cloned.1.call-done = bf16[2,2,4096,128]{3,2,1,0:T(8,128)(2,1)} async-done(((bf16[2,2,512,128]{3,2,1,0:T(8,128)(2,1)}), bf16[2,2,4096,128]{3,2,1,0:T(8,128)(2,1)}) %all-gather.5.cloned.1.call-update) | async-done | bytes 4194320 | tf_op jit(solution)/shard_map/all_gather | solution.py:119
  178.2 8.4 %fusion.20 = bf16[2,2,2,2,8,4,64,128]{7,6,4,5,2,1,0,3:T(8,128)(2,1)S(1)} fusion(bf16[2,2,2,1,4,8,64,128]{7,6,5,4,2,1,0,3:T(8,128)(2,1)} %bitcast.37, bf16[2,2,2,1,4,8,64,128]{7,6,5,4,2,1,0,3:T(8,128)(2,1)} %bitcast.154, pred[]{:T(512)S(6)} %eq.114), kind=kLoop, calls=%fused_computation.30 | loop fusion | flops 12582912 | bytes 16777216 | tf_op jit(solution)/shard_map/transpose | solution.py:129
  186.6 3.1 fusion.59
  189.8 3.0 copy.92
  192.7 3.0 copy.94
  195.7 6.4 %copy.98 = bf16[2,8192,128]{1,2,0:T(8,128)(2,1)} copy(bf16[2,8192,128]{2,1,0:T(8,128)(2,1)} %bitcast.147) | data formatting | bytes 8388608 | tf_op jit(solution)/shard_map/while | solution.py:186
  202.1 41.4 %while.28 = (s32[]{:T(128)}, f32[256,2,2,128]{0,3,2,1:T(8,128)S(1)}, f32[2,2,256]{2,1,0:T(2,128)S(1)}, s32[]{:T(128)}, bf16[2,8192,128]{1,2,0:T(8,128)(2,1)}, /*...) while((s32[]{:T(128)}, ...), condition=%wide.region_7.8_spmd, body=%wide.region_5.7_spmd.sunk | while | flops 272105984 | bytes 4227267 | solution.py:186
  243.6 5.3 %convolution_convert_fusion.1 = bf16[256,4608]{1,0:T(8,128)(2,1)} fusion(bf16[256,512]{0,1:T(8,128)(2,1)S(1)} %bitcast.160, bf16[512,4608]{1,0:T(8,128)(2,1)} %all-gather.7.cloned.1.call-done), kind=kOutput, calls=%fused_computation.32 | convolution fusion | flops 1209139200 | bytes 7340032 | tf_op jit(solution)/shard_map/dot_general | solution.py:191
  248.9 5.8 %all-to-all-start.1 = ((bf16[8,32,4608]{2,1,0:T(8,128)(2,1)}), bf16[8,32,4608]{2,1,0:T(8,128)(2,1)S(1)}, u32[]{:S(2)}, u32[]{:S(2)}) async-start(bf16[8,32,4608]{2,1,0:T(8,128)(2,1)} %bitcast.151), calls=%async_computation.1 | async-start | bytes 4718592 | tf_op jit(solution)/shard_map/all_to_all | solution.py:194
  254.7 42.4 %while.29 = (s32[]{:T(128)}, f32[256,2,2,128]{0,3,2,1:T(8,128)S(1)}, f32[2,2,256]{2,1,0:T(2,128)S(1)}, s32[]{:T(128)}, bf16[2,8192,128]{1,2,0:T(8,128)(2,1)}, /*...) while((s32[]{:T(128)}, ...), condition=%wide.region_13.14_spmd, body=%wide.region_11.13_spmd.sunk | while | flops 272105984 | bytes 4227267 | solution.py:186
  297.2 5.1 %convolution_convert_fusion = bf16[256,4608]{1,0:T(8,128)(2,1)} fusion(bf16[256,512]{0,1:T(8,128)(2,1)S(1)} %bitcast.161, bf16[512,4608]{1,0:T(8,128)(2,1)} %all-gather.7.cloned.1.call-done), kind=kOutput, calls=%fused_computation.31 | convolution fusion | flops 1209139200 | bytes 7340032 | tf_op jit(solution)/shard_map/dot_general | solution.py:191
  302.3 5.7 %all-to-all-start.2 = ((bf16[8,32,4608]{2,1,0:T(8,128)(2,1)}), bf16[8,32,4608]{2,1,0:T(8,128)(2,1)}, u32[]{:S(2)}, u32[]{:S(2)}) async-start(bf16[8,32,4608]{2,1,0:T(8,128)(2,1)} %bitcast.150), calls=%async_computation.2 | async-start | bytes 4718592 | tf_op jit(solution)/shard_map/all_to_all | solution.py:194
  311.9 5.4 %constant_dynamic-slice_fusion = (bf16[1,8192,64]{2,1,0:T(8,128)(2,1)}, bf16[1,8192,64]{2,1,0:T(8,128)(2,1)}) fusion(bf16[2,8192,128]{2,1,0:T(8,128)(2,1)} %bitcast.148, s32[]{:T(128)S(6)} %select_n.276, s32[]{:T(128)S(6)} %select_n.279, bf16[2,8192,128]{2,1,0:T(8,128)(2,1)} %get-tuple-element.661), kind=kLoop, calls=%fused_computation.137 | loop fusion | bytes 4194312 | tf_op jit(solution)/shard_map/dynamic_slice | solution.py:211
  317.3 2.7 copy.100
  320.0 2.7 copy.101
  (281 shorter events, 101.6 us)
Async XLA Ops:
  7.2 1.8 copy-start.3
  7.2 61.0 %all-gather.9.cloned.1.call-start = ((), (), s32[]{:S(2)}) async-start(), calls=%async_computation.5 | async-start | bytes 5898240 | tf_op jit(solution)/shard_map/all_gather | solution.py:79
  9.7 3.2 copy-start.1
  9.7 3.4 %copy-start.5 = (f32[4608]{0:T(1024)S(1)}, f32[4608]{0:T(1024)}, u32[]{:S(2)}) copy-start(f32[4608]{0:T(1024)} %param.15) | copy-start | bytes 55300
  15.9 66.6 %all-to-all-start = ((bf16[8,64,4608]{2,1,0:T(8,128)(2,1)}), bf16[8,64,4608]{2,1,0:T(8,128)(2,1)}, u32[]{:S(2)}, u32[]{:S(2)}) async-start(bf16[8,64,4608]{2,1,0:T(8,128)(2,1)} %broadcast_in_dim.133), calls=%async_computation | async-start | bytes 9437184 | tf_op jit(solution)/shard_map/all_to_all | solution.py:89
  21.0 145.2 %all-gather.5.cloned.1.call-start = ((), (), s32[]{:S(2)}) async-start(), calls=%async_computation.3 | async-start | bytes 4718592 | tf_op jit(solution)/shard_map/all_gather | solution.py:119
  68.1 6.8 %copy-start.7 = (s32[3]{0:T(128)S(1)}, s32[3]{0:T(128)}, u32[]{:S(2)}) copy-start(s32[3]{0:T(128)} %param.21) | copy-start | bytes 40
  68.1 7.0 %copy-start = (s32[8192]{0:T(1024)S(1)}, s32[8192]{0:T(1024)}, u32[]{:S(2)}) copy-start(s32[8192]{0:T(1024)} %param.22) | copy-start | bytes 98308
  74.9 3.4 %copy-start.8 = (s32[3]{0:T(128)S(1)}, s32[3]{0:T(128)}, u32[]{:S(2)}) copy-start(s32[3]{0:T(128)} %param.23) | copy-start | bytes 40
  74.9 13.5 %collective-permute-start = (bf16[4,4608,128]{1,2,0:T(8,128)(2,1)}, bf16[4,4608,128]{1,2,0:T(8,128)(2,1)}, u32[]{:S(2)}, u32[]{:S(2)}) collective-permute-start(bf16[4,4608,128]{1,2,0:T(8,128)(2,1)} %copy.85), channel_id=1, source_target_pairs={{0,32},{32,0},{1,33},{33,1},{2,34},{34,2},{3,35},{35,3},{4,36},{36... | collective-permute-start | bytes 14155784 | tf_op jit(solution)/shard_map/ppermute | solution.py:85
  96.8 146.8 %all-gather.7.cloned.1.call-start = ((), (), s32[]{:S(2)}) async-start(), calls=%async_computation.4 | async-start | bytes 5898240 | tf_op jit(solution)/shard_map/all_gather | solution.py:86
  166.2 12.0 %collective-permute-start.1 = (bf16[2,2,4096,128]{3,2,1,0:T(8,128)(2,1)}, bf16[2,2,4096,128]{3,2,1,0:T(8,128)(2,1)}, u32[]{:S(2)}, u32[]{:S(2)}) collective-permute-start(bf16[2,2,4096,128]{3,2,1,0:T(8,128)(2,1)} %all-gather.5.cloned.1.call-done), channel_id=1, source_target_pairs={{0,32},{32,0},{1,33},{33,1},{2,34},{34,2},{3,35},{35,3},{4,36},{36... | collective-permute-start | bytes 12582920 | tf_op jit(solution)/shard_map/ppermute | solution.py:120
  243.5 5.4 %copy-start.4 = (bf16[2,256,2,2,128]{4,1,3,2,0:T(8,128)(2,1)}, bf16[2,256,2,2,128]{4,1,3,2,0:T(8,128)(2,1)S(1)}, u32[]{:S(2)}) copy-start(bf16[2,256,2,2,128]{4,1,3,2,0:T(8,128)(2,1)S(1)} %get-tuple-element.677) | copy-start | bytes 1572868
  248.9 53.4 %all-to-all-start.1 = ((bf16[8,32,4608]{2,1,0:T(8,128)(2,1)}), bf16[8,32,4608]{2,1,0:T(8,128)(2,1)S(1)}, u32[]{:S(2)}, u32[]{:S(2)}) async-start(bf16[8,32,4608]{2,1,0:T(8,128)(2,1)} %bitcast.151), calls=%async_computation.1 | async-start | bytes 4718592 | tf_op jit(solution)/shard_map/all_to_all | solution.py:194
  302.3 24.8 %all-to-all-start.2 = ((bf16[8,32,4608]{2,1,0:T(8,128)(2,1)}), bf16[8,32,4608]{2,1,0:T(8,128)(2,1)}, u32[]{:S(2)}, u32[]{:S(2)}) async-start(bf16[8,32,4608]{2,1,0:T(8,128)(2,1)} %bitcast.150), calls=%async_computation.2 | async-start | bytes 4718592 | tf_op jit(solution)/shard_map/all_to_all | solution.py:194
  327.1 2.1 copy-start.2
  327.1 2.3 copy-start.6
Sparse Core Ops, SparseCore 0:
  13.0 55.1 all-gather.8
  96.9 69.2 all-gather.4
  167.8 52.9 all-gather.6

commit v2 on v0

--- a/solution.py
+++ b/solution.py
@@ -14,7 +14,7 @@
 SCORE_SHIFT = 20.0
 ROPE_BASE = 10000.0
 KEY_TILE = 512
-Q_CHUNKS = 2
+Q_CHUNKS = 4
 HEADS_PER_DEVICE = 4
 
 

time: 313 us -> 381 us (1.22)
  the two profiles are of different devices: /device:TPU:7 before, /device:TPU:4 now
where the time goes in v2:
time: 381 us; the launch traced here: 378 us
  matrix products  136 us (36%)
  waiting for transfers between devices  98.8 us (26%)
  local copies, waits for them, and re-layouts  47.7 us (13%)
  between operations  36.3 us (10%)
  other arithmetic  29.5 us (8%)
  starting transfers between devices  27.4 us (7%)
    dot_general x40, matrix products, tile(): jnp.einsum('qkgd,ktd->kgqt', q_chunks[chunk], k_block, preferred_element_...  59.2 us
    dot_general x40, matrix products, tile(): jnp.einsum('kgqt,ktd->qkgd', weights.astype(jnp.bfloat16), v_block, prefe...  48.4 us
    all_gather x1, waiting for transfers between devices, on_device(): lax.all_gather(jnp.where(core == 0, query_weight, jnp.concatenate([key_we...  47.1 us
    all_gather x1, waiting for transfers between devices, on_device(): kv_all = lax.all_gather(kv, ('seq', 'tl'), axis=2, tiled=True)  43.8 us
    all_to_all x4, starting transfers between devices, attend(): lax.all_to_all(partial.reshape(n_group, member_part, -1), 'th', 0, 0, til...  22 us
    dot_general x4, matrix products, attend(): jnp.dot(attended, pair_out, preferred_element_type=jnp.float32)  16.7 us
    unnamed x2, matrix products  11.8 us
    and x40, other arithmetic, tile(): (k_ids[None, :] <= q_ids[chunk][:, None]) & (k_segs[None, :] == q_segs[ch...  8.08 us
  transfers between devices with their start and end apart: 9, of which 3 were waited for; matrix products, arithmetic and copies ran while one was open for 50% of the time, Pallas kernels for 0%

profile of v2, /device:TPU:4, one launch (start us, length us, event | category | flops | bytes accessed | tf_op | source)
XLA Modules:
  0.0 377.9 jit_solution(16639012413430296657)
XLA Ops:
  10.3 3.5 maximum_select_fusion.1
  16.8 5.1 %all-to-all-start = ((bf16[8,64,4608]{2,1,0:T(8,128)(2,1)}), bf16[8,64,4608]{2,1,0:T(8,128)(2,1)}, u32[]{:S(2)}, u32[]{:S(2)}) async-start(bf16[8,64,4608]{2,1,0:T(8,128)(2,1)} %broadcast_in_dim.171), calls=%async_computation | async-start | bytes 9437184 | tf_op jit(solution)/shard_map/all_to_all | solution.py:89
  22.0 47.1 %all-gather.9.cloned.1.call-done = bf16[18432,128]{1,0:T(8,128)(2,1)} async-done(((bf16[4608,128]{1,0:T(8,128)(2,1)}), bf16[18432,128]{1,0:T(8,128)(2,1)}) %all-gather.9.cloned.1.call-update) | async-done | bytes 4718608 | tf_op jit(solution)/shard_map/all_gather | solution.py:79
  69.1 6.8 %copy.98 = bf16[4,4608,128]{1,2,0:T(8,128)(2,1)} copy(bf16[4,4608,128]{2,1,0:T(8,128)(2,1)} %bitcast.249) | data formatting | bytes 9437184 | tf_op jit(solution)/shard_map/all_gather | solution.py:79
  76.1 3.1 gather_fusion
  83.5 5.9 %fusion.127 = f32[512,512]{0,1:S(1)} fusion(bf16[512,4608]{1,0:T(8,128)(2,1)} %bitcast.40, bf16[4608,512]{0,1:T(8,128)(2,1)} %bitcast.248), kind=kOutput, calls=%fused_computation.259 | convolution fusion | flops 2415919104 | bytes 10485760
  89.4 5.9 %fusion.128 = f32[512,512]{0,1:S(1)} fusion(bf16[512,4608]{1,0:T(8,128)(2,1)} %bitcast.40, bf16[4608,512]{0,1:T(8,128)(2,1)} %bitcast.46), kind=kOutput, calls=%fused_computation.260 | convolution fusion | flops 2415919104 | bytes 10485760
  124.9 43.8 %all-gather.5.cloned.1.call-done = bf16[2,2,8192,128]{3,2,1,0:T(8,128)(2,1)} async-done(((bf16[2,2,512,128]{3,2,1,0:T(8,128)(2,1)}), bf16[2,2,8192,128]{3,2,1,0:T(8,128)(2,1)}) %all-gather.5.cloned.1.call-update) | async-done | bytes 8388624 | tf_op jit(solution)/shard_map/all_gather | solution.py:119
  168.8 4.4 %fusion.125 = (bf16[1,2,4,8,4,64,128]{6,5,3,4,2,1,0:T(8,128)(2,1)S(1)}, bf16[1,2,4,8,4,64,128]{6,5,3,4,2,1,0:T(8,128)(2,1)S(1)}) fusion(bf16[2,2,4,8,4,64,128]{6,5,3,4,2,1,0:T(8,128)(2,1)} %bitcast.247), kind=kLoop, calls=%fused_computation.257 | loop fusion | bytes 16777216 | tf_op jit(solution)/shard_map/slice | solution.py:122
  179.0 6.5 %copy.111 = bf16[2,8192,128]{1,2,0:T(8,128)(2,1)} copy(bf16[2,8192,128]{2,1,0:T(8,128)(2,1)} %bitcast.244) | data formatting | bytes 8388608 | tf_op jit(solution)/shard_map/while | solution.py:176
  185.6 30.4 %while.56 = (s32[]{:T(128)}, f32[128,2,2,128]{0,3,2,1:T(8,128)S(1)}, f32[2,2,128]{2,1,0:T(2,128)S(1)}, s32[]{:T(128)}, bf16[2,8192,128]{1,2,0:T(8,128)(2,1)}, /*...) while((s32[]{:T(128)}, ...), condition=%wide.region_7.8_spmd, body=%wide.region_5.7_spmd.sunk | while | flops 136053248 | bytes 2380995 | solution.py:176
  216.0 7.3 %all-gather.7.cloned.1.call-done = bf16[512,4608]{1,0:T(8,128)(2,1)} async-done(((bf16[128,4608]{1,0:T(8,128)(2,1)}), bf16[512,4608]{1,0:T(8,128)(2,1)}) %all-gather.7.cloned.1.call-update) | async-done | bytes 4718608 | tf_op jit(solution)/shard_map/all_gather | solution.py:86
  223.4 4.2 %convolution_convert_fusion.3 = bf16[128,4608]{1,0:T(8,128)(2,1)} fusion(bf16[128,512]{0,1:T(8,128)(2,1)S(1)} %bitcast.263, bf16[512,4608]{1,0:T(8,128)(2,1)} %all-gather.7.cloned.1.call-done), kind=kOutput, calls=%fused_computation.92 | convolution fusion | flops 604569600 | bytes 6029312 | tf_op jit(solution)/shard_map/dot_general | solution.py:181
  227.5 4.9 %all-to-all-start.1 = ((bf16[8,16,4608]{2,1,0:T(8,128)(2,1)}), bf16[8,16,4608]{2,1,0:T(8,128)(2,1)S(1)}, u32[]{:S(2)}, u32[]{:S(2)}) async-start(bf16[8,16,4608]{2,1,0:T(8,128)(2,1)} %bitcast.252), calls=%async_computation.1 | async-start | bytes 2359296 | tf_op jit(solution)/shard_map/all_to_all | solution.py:184
  232.5 30.4 %while.57 = (s32[]{:T(128)}, f32[128,2,2,128]{0,3,2,1:T(8,128)S(1)}, f32[2,2,128]{2,1,0:T(2,128)S(1)}, s32[]{:T(128)}, bf16[2,8192,128]{1,2,0:T(8,128)(2,1)}, /*...) while((s32[]{:T(128)}, ...), condition=%wide.region_13.14_spmd, body=%wide.region_11.13_spmd.sunk | while | flops 136053248 | bytes 2380995 | solution.py:176
  262.9 4.2 %convolution_convert_fusion.2 = bf16[128,4608]{1,0:T(8,128)(2,1)} fusion(bf16[128,512]{0,1:T(8,128)(2,1)S(1)} %bitcast.265, bf16[512,4608]{1,0:T(8,128)(2,1)} %all-gather.7.cloned.1.call-done), kind=kOutput, calls=%fused_computation.91 | convolution fusion | flops 604569600 | bytes 6029312 | tf_op jit(solution)/shard_map/dot_general | solution.py:181
  267.0 5.7 %all-to-all-start.2 = ((bf16[8,16,4608]{2,1,0:T(8,128)(2,1)}), bf16[8,16,4608]{2,1,0:T(8,128)(2,1)}, u32[]{:S(2)}, u32[]{:S(2)}) async-start(bf16[8,16,4608]{2,1,0:T(8,128)(2,1)} %bitcast.251), calls=%async_computation.2 | async-start | bytes 2359296 | tf_op jit(solution)/shard_map/all_to_all | solution.py:184
  272.8 30.4 %while.58 = (s32[]{:T(128)}, f32[128,2,2,128]{0,3,2,1:T(8,128)S(1)}, f32[2,2,128]{2,1,0:T(2,128)S(1)}, s32[]{:T(128)}, bf16[2,8192,128]{1,2,0:T(8,128)(2,1)}, /*...) while((s32[]{:T(128)}, ...), condition=%wide.region_19.20_spmd, body=%wide.region_17.19_spmd.sunk | while | flops 136053248 | bytes 2380995 | solution.py:176
  303.2 4.2 %convolution_convert_fusion.1 = bf16[128,4608]{1,0:T(8,128)(2,1)} fusion(bf16[128,512]{0,1:T(8,128)(2,1)S(1)} %bitcast.266, bf16[512,4608]{1,0:T(8,128)(2,1)} %all-gather.7.cloned.1.call-done), kind=kOutput, calls=%fused_computation.90 | convolution fusion | flops 604569600 | bytes 6029312 | tf_op jit(solution)/shard_map/dot_general | solution.py:181
  307.4 5.7 %all-to-all-start.3 = ((bf16[8,16,4608]{2,1,0:T(8,128)(2,1)}), bf16[8,16,4608]{2,1,0:T(8,128)(2,1)S(1)}, u32[]{:S(2)}, u32[]{:S(2)}) async-start(bf16[8,16,4608]{2,1,0:T(8,128)(2,1)} %bitcast.250), calls=%async_computation.3 | async-start | bytes 2359296 | tf_op jit(solution)/shard_map/all_to_all | solution.py:184
  313.1 30.3 %while.59 = (s32[]{:T(128)}, f32[128,2,2,128]{0,3,2,1:T(8,128)S(1)}, f32[2,2,128]{2,1,0:T(2,128)S(1)}, s32[]{:T(128)}, bf16[2,8192,128]{1,2,0:T(8,128)(2,1)}, /*...) while((s32[]{:T(128)}, ...), condition=%wide.region_25.26_spmd, body=%wide.region_23.25_spmd.sunk | while | flops 136053248 | bytes 2380995 | solution.py:176
  343.5 4.2 %convolution_convert_fusion = bf16[128,4608]{1,0:T(8,128)(2,1)} fusion(bf16[128,512]{0,1:T(8,128)(2,1)S(1)} %bitcast.264, bf16[512,4608]{1,0:T(8,128)(2,1)} %all-gather.7.cloned.1.call-done), kind=kOutput, calls=%fused_computation.89 | convolution fusion | flops 604569600 | bytes 6029312 | tf_op jit(solution)/shard_map/dot_general | solution.py:181
  348.7 5.7 %all-to-all-start.4 = ((bf16[8,16,4608]{2,1,0:T(8,128)(2,1)}), bf16[8,16,4608]{2,1,0:T(8,128)(2,1)}, u32[]{:S(2)}, u32[]{:S(2)}) async-start(bf16[8,16,4608]{2,1,0:T(8,128)(2,1)} %bitcast.253), calls=%async_computation.4 | async-start | bytes 2359296 | tf_op jit(solution)/shard_map/all_to_all | solution.py:184
  354.4 4.8 %constant_dynamic-slice_fusion = (bf16[1,8192,64]{2,1,0:T(8,128)(2,1)S(1)}, bf16[1,8192,64]{2,1,0:T(8,128)(2,1)}) fusion(bf16[2,8192,128]{2,1,0:T(8,128)(2,1)} %bitcast.245, s32[]{:T(128)S(6)} %select_n.315, s32[]{:T(128)S(6)} %select_n.318, bf16[2,8192,128]{2,1,0:T(8,128)(2,1)} %get-tuple-element.1304), kind=kLoop, calls=%fused_computation.231 | loop fusion | bytes 4194312 | tf_op jit(solution)/shard_map/dynamic_slice | solution.py:201
  (386 shorter events, 156.5 us)
Async XLA Ops:
  7.2 1.8 copy-start.6
  7.2 61.9 %all-gather.9.cloned.1.call-start = ((), (), s32[]{:S(2)}) async-start(), calls=%async_computation.7 | async-start | bytes 5898240 | tf_op jit(solution)/shard_map/all_gather | solution.py:79
  10.3 3.5 copy-start.1
  10.3 3.8 copy-start.7
  16.8 66.6 %all-to-all-start = ((bf16[8,64,4608]{2,1,0:T(8,128)(2,1)}), bf16[8,64,4608]{2,1,0:T(8,128)(2,1)}, u32[]{:S(2)}, u32[]{:S(2)}) async-start(bf16[8,64,4608]{2,1,0:T(8,128)(2,1)} %broadcast_in_dim.171), calls=%async_computation | async-start | bytes 9437184 | tf_op jit(solution)/shard_map/all_to_all | solution.py:89
  21.9 146.8 %all-gather.5.cloned.1.call-start = ((), (), s32[]{:S(2)}) async-start(), calls=%async_computation.5 | async-start | bytes 8912896 | tf_op jit(solution)/shard_map/all_gather | solution.py:119
  69.1 6.8 %copy-start.9 = (s32[3]{0:T(128)S(1)}, s32[3]{0:T(128)}, u32[]{:S(2)}) copy-start(s32[3]{0:T(128)} %param.25) | copy-start | bytes 40
  69.1 7.0 %copy-start = (s32[8192]{0:T(1024)S(1)}, s32[8192]{0:T(1024)}, u32[]{:S(2)}) copy-start(s32[8192]{0:T(1024)} %param.26) | copy-start | bytes 98308
  75.9 3.4 copy-start.10
  75.9 13.5 %collective-permute-start = (bf16[4,4608,128]{1,2,0:T(8,128)(2,1)}, bf16[4,4608,128]{1,2,0:T(8,128)(2,1)}, u32[]{:S(2)}, u32[]{:S(2)}) collective-permute-start(bf16[4,4608,128]{1,2,0:T(8,128)(2,1)} %copy.98), channel_id=1, source_target_pairs={{0,32},{32,0},{64,96},{96,64},{1,33},{33,1},{65,97},{97,65},{2,34}... | collective-permute-start | bytes 14155784 | tf_op jit(solution)/shard_map/ppermute | solution.py:85
  97.8 125.6 %all-gather.7.cloned.1.call-start = ((), (), s32[]{:S(2)}) async-start(), calls=%async_computation.6 | async-start | bytes 5898240 | tf_op jit(solution)/shard_map/all_gather | solution.py:86
  227.5 39.5 %all-to-all-start.1 = ((bf16[8,16,4608]{2,1,0:T(8,128)(2,1)}), bf16[8,16,4608]{2,1,0:T(8,128)(2,1)S(1)}, u32[]{:S(2)}, u32[]{:S(2)}) async-start(bf16[8,16,4608]{2,1,0:T(8,128)(2,1)} %bitcast.252), calls=%async_computation.1 | async-start | bytes 2359296 | tf_op jit(solution)/shard_map/all_to_all | solution.py:184
  267.0 5.7 %copy-start.2 = (bf16[8,16,4608]{2,1,0:T(8,128)(2,1)}, bf16[8,16,4608]{2,1,0:T(8,128)(2,1)S(1)}, u32[]{:S(2)}) copy-start(bf16[8,16,4608]{2,1,0:T(8,128)(2,1)S(1)} %all-to-all-done.1) | copy-start | bytes 3538948
  267.0 40.3 %all-to-all-start.2 = ((bf16[8,16,4608]{2,1,0:T(8,128)(2,1)}), bf16[8,16,4608]{2,1,0:T(8,128)(2,1)}, u32[]{:S(2)}, u32[]{:S(2)}) async-start(bf16[8,16,4608]{2,1,0:T(8,128)(2,1)} %bitcast.251), calls=%async_computation.2 | async-start | bytes 2359296 | tf_op jit(solution)/shard_map/all_to_all | solution.py:184
  307.4 40.3 %all-to-all-start.3 = ((bf16[8,16,4608]{2,1,0:T(8,128)(2,1)}), bf16[8,16,4608]{2,1,0:T(8,128)(2,1)S(1)}, u32[]{:S(2)}, u32[]{:S(2)}) async-start(bf16[8,16,4608]{2,1,0:T(8,128)(2,1)} %bitcast.250), calls=%async_computation.3 | async-start | bytes 2359296 | tf_op jit(solution)/shard_map/all_to_all | solution.py:184
  347.7 1.0 copy-start.4
  348.7 19.9 %all-to-all-start.4 = ((bf16[8,16,4608]{2,1,0:T(8,128)(2,1)}), bf16[8,16,4608]{2,1,0:T(8,128)(2,1)}, u32[]{:S(2)}, u32[]{:S(2)}) async-start(bf16[8,16,4608]{2,1,0:T(8,128)(2,1)} %bitcast.253), calls=%async_computation.4 | async-start | bytes 2359296 | tf_op jit(solution)/shard_map/all_to_all | solution.py:184
  363.5 3.3 copy-start.3
  365.2 3.2 copy-start.5
  368.5 1.8 copy-start.8
Sparse Core Ops, SparseCore 0:
  13.9 55.1 all-gather.8
  97.9 70.8 all-gather.4
  170.4 52.8 all-gather.6

commit v3 on v0

--- a/solution.py
+++ b/solution.py
@@ -13,7 +13,7 @@
 QUERY_SCALE = 144.0 ** (-0.5)
 SCORE_SHIFT = 20.0
 ROPE_BASE = 10000.0
-KEY_TILE = 512
+KEY_TILE = 1024
 Q_CHUNKS = 2
 HEADS_PER_DEVICE = 4
 

time: 313 us -> 311 us (level)
  the two profiles are of different devices: /device:TPU:7 before, /device:TPU:4 now
where the time goes in v3:
time: 311 us; the launch traced here: 306 us
  waiting for transfers between devices  142 us (46%)
  matrix products  53.1 us (17%)
  local copies, waits for them, and re-layouts  46.2 us (15%)
  between operations  25.8 us (8%)
  other arithmetic  23.2 us (7%)
  starting transfers between devices  14.7 us (5%)
    all_gather x1, waiting for transfers between devices, on_device(): kv_all = lax.all_gather(kv, ('seq', 'tl'), axis=2, tiled=True)  58.3 us
    all_gather x1, waiting for transfers between devices, on_device(): lax.all_gather(jnp.where(core == 0, query_weight, jnp.concatenate([key_we...  47.1 us
    all_gather x1, waiting for transfers between devices, on_device(): pair_out = lax.all_gather(out_weight, 'tl', axis=0, tiled=True)  20.2 us
    all_to_all x2, waiting for transfers between devices, attend(): lax.all_to_all(partial.reshape(n_group, member_part, -1), 'th', 0, 0, til...  16.2 us
    dot_general x6, matrix products, tile(): jnp.einsum('kgqt,ktd->qkgd', weights.astype(jnp.bfloat16), v_block, prefe...  15.6 us
    dot_general x6, matrix products, tile(): jnp.einsum('qkgd,ktd->kgqt', q_chunks[chunk], k_block, preferred_element_...  15.3 us
    unnamed x2, matrix products  11.9 us
    dot_general x2, matrix products, attend(): jnp.dot(attended, pair_out, preferred_element_type=jnp.float32)  10.3 us
  transfers between devices with their start and end apart: 7, of which 5 were waited for; matrix products, arithmetic and copies ran while one was open for 32% of the time, Pallas kernels for 0%

profile of v3, /device:TPU:4, one launch (start us, length us, event | category | flops | bytes accessed | tf_op | source)
XLA Modules:
  0.0 306.1 jit_solution(14744435461499649008)
XLA Ops:
  10.6 3.1 %maximum_select_fusion.1 = bf16[4608,128]{1,0:T(8,128)(2,1)} fusion(bf16[4608,128]{1,0:T(8,128)(2,1)} %param.16, bf16[4608,64]{1,0:T(8,128)(2,1)S(1)} %copy.81, bf16[4608,64]{1,0:T(8,128)(2,1)S(1)} %copy.80, pred[]{:T(512)S(6)} %eq.114), kind=kLoop, calls=%fused_computation.63 | loop fusion | flops 2949120 | bytes 3538945 | tf_op jit(solution)/shard_map/jit(_where)/select_n | solution.py:80
  16.7 5.1 %all-to-all-start = ((bf16[8,64,4608]{2,1,0:T(8,128)(2,1)}), bf16[8,64,4608]{2,1,0:T(8,128)(2,1)}, u32[]{:S(2)}, u32[]{:S(2)}) async-start(bf16[8,64,4608]{2,1,0:T(8,128)(2,1)} %broadcast_in_dim.133), calls=%async_computation | async-start | bytes 9437184 | tf_op jit(solution)/shard_map/all_to_all | solution.py:89
  21.9 47.1 %all-gather.9.cloned.1.call-done = bf16[18432,128]{1,0:T(8,128)(2,1)} async-done(((bf16[4608,128]{1,0:T(8,128)(2,1)}), bf16[18432,128]{1,0:T(8,128)(2,1)}) %all-gather.9.cloned.1.call-update) | async-done | bytes 4718608 | tf_op jit(solution)/shard_map/all_gather | solution.py:79
  69.0 6.8 %copy.82 = bf16[4,4608,128]{1,2,0:T(8,128)(2,1)} copy(bf16[4,4608,128]{2,1,0:T(8,128)(2,1)} %bitcast.173) | data formatting | bytes 9437184 | tf_op jit(solution)/shard_map/all_gather | solution.py:79
  76.0 3.1 %gather_fusion = s32[512]{0:T(512)S(1)} fusion(s32[8192]{0:T(1024)S(1)} %copy-done, s32[1024]{0:T(1024)S(1)} %pad_clamp_fusion), kind=kCustom, calls=%fused_computation | custom fusion | bytes 6144 | tf_op jit(solution)/shard_map/jit(_take)/gather | solution.py:111
  83.3 5.9 %fusion.86 = f32[512,512]{0,1:S(1)} fusion(bf16[512,4608]{1,0:T(8,128)(2,1)} %bitcast.22, bf16[4608,512]{0,1:T(8,128)(2,1)} %bitcast.172), kind=kOutput, calls=%fused_computation.174 | convolution fusion | flops 2415919104 | bytes 10485760
  89.3 5.9 %fusion.87 = f32[512,512]{0,1:S(1)} fusion(bf16[512,4608]{1,0:T(8,128)(2,1)} %bitcast.22, bf16[4608,512]{0,1:T(8,128)(2,1)} %bitcast.28), kind=kOutput, calls=%fused_computation.175 | convolution fusion | flops 2415919104 | bytes 10485760
  110.3 58.3 %all-gather.5.cloned.1.call-done = bf16[2,2,8192,128]{3,2,1,0:T(8,128)(2,1)} async-done(((bf16[2,2,512,128]{3,2,1,0:T(8,128)(2,1)}), bf16[2,2,8192,128]{3,2,1,0:T(8,128)(2,1)}) %all-gather.5.cloned.1.call-update) | async-done | bytes 8388624 | tf_op jit(solution)/shard_map/all_gather | solution.py:119
  168.6 4.4 %fusion.84 = (bf16[1,2,4,8,4,64,128]{6,5,3,4,2,1,0:T(8,128)(2,1)S(1)}, bf16[1,2,4,8,4,64,128]{6,5,3,4,2,1,0:T(8,128)(2,1)S(1)}) fusion(bf16[2,2,4,8,4,64,128]{6,5,3,4,2,1,0:T(8,128)(2,1)} %bitcast.171), kind=kLoop, calls=%fused_computation.172 | loop fusion | bytes 16777216 | tf_op jit(solution)/shard_map/slice | solution.py:122
  173.0 2.9 copy.89
  175.9 2.9 copy.91
  178.9 6.5 %copy.95 = bf16[2,8192,128]{1,2,0:T(8,128)(2,1)} copy(bf16[2,8192,128]{2,1,0:T(8,128)(2,1)} %bitcast.166) | data formatting | bytes 8388608 | tf_op jit(solution)/shard_map/while | solution.py:176
  185.4 16.7 %while.28 = (s32[]{:T(128)}, f32[256,2,2,128]{0,3,2,1:T(8,128)S(1)}, f32[2,2,256]{2,1,0:T(2,128)S(1)}, s32[]{:T(128)}, bf16[2,8192,128]{1,2,0:T(8,128)(2,1)}, /*...) while((s32[]{:T(128)}, ...), condition=%wide.region_7.8_spmd, body=%wide.region_5.7_spmd.sunk | while | flops 548275200 | bytes 11577539 | solution.py:176
  203.0 20.2 %all-gather.7.cloned.1.call-done = bf16[512,4608]{1,0:T(8,128)(2,1)} async-done(((bf16[128,4608]{1,0:T(8,128)(2,1)}), bf16[512,4608]{1,0:T(8,128)(2,1)}) %all-gather.7.cloned.1.call-update) | async-done | bytes 4718608 | tf_op jit(solution)/shard_map/all_gather | solution.py:86
  223.2 5.2 %convolution_convert_fusion.1 = bf16[256,4608]{1,0:T(8,128)(2,1)} fusion(bf16[256,512]{0,1:T(8,128)(2,1)S(1)} %bitcast.179, bf16[512,4608]{1,0:T(8,128)(2,1)} %all-gather.7.cloned.1.call-done), kind=kOutput, calls=%fused_computation.46 | convolution fusion | flops 1209139200 | bytes 7340032 | tf_op jit(solution)/shard_map/dot_general | solution.py:181
  228.4 4.9 %all-to-all-start.1 = ((bf16[8,32,4608]{2,1,0:T(8,128)(2,1)}), bf16[8,32,4608]{2,1,0:T(8,128)(2,1)S(1)}, u32[]{:S(2)}, u32[]{:S(2)}) async-start(bf16[8,32,4608]{2,1,0:T(8,128)(2,1)} %bitcast.170), calls=%async_computation.1 | async-start | bytes 4718592 | tf_op jit(solution)/shard_map/all_to_all | solution.py:184
  233.3 17.1 %while.29 = (s32[]{:T(128)}, f32[256,2,2,128]{0,3,2,1:T(8,128)S(1)}, f32[2,2,256]{2,1,0:T(2,128)S(1)}, s32[]{:T(128)}, bf16[2,8192,128]{1,2,0:T(8,128)(2,1)}, /*...) while((s32[]{:T(128)}, ...), condition=%wide.region_13.14_spmd, body=%wide.region_11.13_spmd.sunk | while | flops 548275200 | bytes 11577539 | solution.py:176
  250.5 5.1 %convolution_convert_fusion = bf16[256,4608]{1,0:T(8,128)(2,1)} fusion(bf16[256,512]{0,1:T(8,128)(2,1)S(1)} %bitcast.180, bf16[512,4608]{1,0:T(8,128)(2,1)} %all-gather.7.cloned.1.call-done), kind=kOutput, calls=%fused_computation.45 | convolution fusion | flops 1209139200 | bytes 7340032 | tf_op jit(solution)/shard_map/dot_general | solution.py:181
  255.6 7.2 %all-to-all-done.1 = bf16[8,32,4608]{2,1,0:T(8,128)(2,1)S(1)} async-done(((bf16[8,32,4608]{2,1,0:T(8,128)(2,1)}), bf16[8,32,4608]{2,1,0:T(8,128)(2,1)S(1)}, u32[]{:S(2)}, u32[]{:S(2)}) %all-to-all-start.1) | async-done | bytes 2359328 | tf_op jit(solution)/shard_map/all_to_all | solution.py:184
  262.9 4.4 %all-to-all-start.2 = ((bf16[8,32,4608]{2,1,0:T(8,128)(2,1)}), bf16[8,32,4608]{2,1,0:T(8,128)(2,1)}, u32[]{:S(2)}, u32[]{:S(2)}) async-start(bf16[8,32,4608]{2,1,0:T(8,128)(2,1)} %bitcast.169), calls=%async_computation.2 | async-start | bytes 4718592 | tf_op jit(solution)/shard_map/all_to_all | solution.py:184
  271.2 5.3 %constant_dynamic-slice_fusion = (bf16[1,8192,64]{2,1,0:T(8,128)(2,1)}, bf16[1,8192,64]{2,1,0:T(8,128)(2,1)}) fusion(bf16[2,8192,128]{2,1,0:T(8,128)(2,1)} %bitcast.167, s32[]{:T(128)S(6)} %select_n.271, s32[]{:T(128)S(6)} %select_n.274, bf16[2,8192,128]{2,1,0:T(8,128)(2,1)} %get-tuple-element.656), kind=kLoop, calls=%fused_computation.151 | loop fusion | bytes 4194312 | tf_op jit(solution)/shard_map/dynamic_slice | solution.py:201
  276.5 2.7 copy.97
  279.2 2.7 copy.98
  286.2 9.0 %all-to-all-done.2 = bf16[8,32,4608]{2,1,0:T(8,128)(2,1)} async-done(((bf16[8,32,4608]{2,1,0:T(8,128)(2,1)}), bf16[8,32,4608]{2,1,0:T(8,128)(2,1)}, u32[]{:S(2)}, u32[]{:S(2)}) %all-to-all-start.2) | async-done | bytes 2359328 | tf_op jit(solution)/shard_map/all_to_all | solution.py:184
  (132 shorter events, 60.6 us)
Async XLA Ops:
  7.2 61.8 %all-gather.9.cloned.1.call-start = ((), (), s32[]{:S(2)}) async-start(), calls=%async_computation.5 | async-start | bytes 5898240 | tf_op jit(solution)/shard_map/all_gather | solution.py:79
  8.9 4.8 %copy-start.1 = (bf16[64,4608]{1,0:T(8,128)(2,1)S(1)}, bf16[64,4608]{1,0:T(8,128)(2,1)}, u32[]{:S(2)}) copy-start(bf16[64,4608]{1,0:T(8,128)(2,1)} %param.14) | copy-start | bytes 1769476
  8.9 5.1 %copy-start.4 = (f32[4608]{0:T(1024)S(1)}, f32[4608]{0:T(1024)}, u32[]{:S(2)}) copy-start(f32[4608]{0:T(1024)} %param.15) | copy-start | bytes 55300
  16.7 66.6 %all-to-all-start = ((bf16[8,64,4608]{2,1,0:T(8,128)(2,1)}), bf16[8,64,4608]{2,1,0:T(8,128)(2,1)}, u32[]{:S(2)}, u32[]{:S(2)}) async-start(bf16[8,64,4608]{2,1,0:T(8,128)(2,1)} %broadcast_in_dim.133), calls=%async_computation | async-start | bytes 9437184 | tf_op jit(solution)/shard_map/all_to_all | solution.py:89
  21.8 146.8 %all-gather.5.cloned.1.call-start = ((), (), s32[]{:S(2)}) async-start(), calls=%async_computation.3 | async-start | bytes 8912896 | tf_op jit(solution)/shard_map/all_gather | solution.py:119
  69.0 6.8 %copy-start.6 = (s32[3]{0:T(128)S(1)}, s32[3]{0:T(128)}, u32[]{:S(2)}) copy-start(s32[3]{0:T(128)} %param.21) | copy-start | bytes 40
  69.0 7.0 %copy-start = (s32[8192]{0:T(1024)S(1)}, s32[8192]{0:T(1024)}, u32[]{:S(2)}) copy-start(s32[8192]{0:T(1024)} %param.22) | copy-start | bytes 98308
  69.0 10.2 %copy-start.7 = (s32[3]{0:T(128)S(1)}, s32[3]{0:T(128)}, u32[]{:S(2)}) copy-start(s32[3]{0:T(128)} %param.23) | copy-start | bytes 40
  75.8 13.5 %collective-permute-start = (bf16[4,4608,128]{1,2,0:T(8,128)(2,1)}, bf16[4,4608,128]{1,2,0:T(8,128)(2,1)}, u32[]{:S(2)}, u32[]{:S(2)}) collective-permute-start(bf16[4,4608,128]{1,2,0:T(8,128)(2,1)} %copy.82), channel_id=1, source_target_pairs={{0,32},{32,0},{64,96},{96,64},{1,33},{33,1},{65,97},{97,65},{2,34}... | collective-permute-start | bytes 14155784 | tf_op jit(solution)/shard_map/ppermute | solution.py:85
  97.6 125.6 %all-gather.7.cloned.1.call-start = ((), (), s32[]{:S(2)}) async-start(), calls=%async_computation.4 | async-start | bytes 5898240 | tf_op jit(solution)/shard_map/all_gather | solution.py:86
  202.2 0.8 copy-start.3
  228.4 34.5 %all-to-all-start.1 = ((bf16[8,32,4608]{2,1,0:T(8,128)(2,1)}), bf16[8,32,4608]{2,1,0:T(8,128)(2,1)S(1)}, u32[]{:S(2)}, u32[]{:S(2)}) async-start(bf16[8,32,4608]{2,1,0:T(8,128)(2,1)} %bitcast.170), calls=%async_computation.1 | async-start | bytes 4718592 | tf_op jit(solution)/shard_map/all_to_all | solution.py:184
  262.9 32.3 %all-to-all-start.2 = ((bf16[8,32,4608]{2,1,0:T(8,128)(2,1)}), bf16[8,32,4608]{2,1,0:T(8,128)(2,1)}, u32[]{:S(2)}, u32[]{:S(2)}) async-start(bf16[8,32,4608]{2,1,0:T(8,128)(2,1)} %bitcast.169), calls=%async_computation.2 | async-start | bytes 4718592 | tf_op jit(solution)/shard_map/all_to_all | solution.py:184
  283.5 15.0 %copy-start.5 = (f32[4608]{0:T(1024)S(1)}, f32[4608]{0:T(1024)}, u32[]{:S(2)}) copy-start(f32[4608]{0:T(1024)} %param.20) | copy-start | bytes 55300
  286.2 12.3 %copy-start.2 = (f32[32,4608]{1,0:T(8,128)S(1)}, f32[32,4608]{1,0:T(8,128)}, u32[]{:S(2)}) copy-start(f32[32,4608]{1,0:T(8,128)} %convert_reduce_fusion.1) | copy-start | bytes 1769476
Sparse Core Ops, SparseCore 0:
  13.8 55.1 all-gather.8
  97.7 70.8 all-gather.4
  170.3 52.8 all-gather.6

commit v4 on v3

--- a/solution.py
+++ b/solution.py
@@ -13,7 +13,7 @@
 QUERY_SCALE = 144.0 ** (-0.5)
 SCORE_SHIFT = 20.0
 ROPE_BASE = 10000.0
-KEY_TILE = 1024
+KEY_TILE = 2048
 Q_CHUNKS = 2
 HEADS_PER_DEVICE = 4
 

time: 311 us -> 309 us (level)
  waiting for transfers between devices: 142 us -> 120 us
  matrix products: 53.1 us -> 70.1 us
  other arithmetic: 23.2 us -> 29.8 us
    all_gather x1, waiting for transfers between devices: 20.2 us -> 9.01 us  [on_device(): pair_out = lax.all_gather(out_weight, 'tl', axis=0, tiled=True)]
    all_to_all x2, waiting for transfers between devices: 16.2 us -> 5.06 us  [attend(): lax.all_to_all(partial.reshape(n_group, member_part, -1), 'th', 0, 0, til...]
    dot_general x6, matrix products: 15.3 us -> 24.1 us  [tile(): jnp.einsum('qkgd,ktd->kgqt', q_chunks[chunk], k_block, preferred_element_...]
    dot_general x6, matrix products: 15.6 us -> 23.8 us  [tile(): jnp.einsum('kgqt,ktd->qkgd', weights.astype(jnp.bfloat16), v_block, prefe...]
    and x6, other arithmetic: 2.04 us -> 8.69 us  [tile(): (k_ids[None, :] <= q_ids[chunk][:, None]) & (k_segs[None, :] == q_segs[ch...]
  transfers between devices with their start and end apart: 7 -> 7, of which waited for: 5 -> 4; matrix products, arithmetic and copies ran while one was open for 32% -> 39% of each run, Pallas kernels for 0% -> 0%
where the time goes in v4:
time: 309 us; the launch traced here: 307 us
  waiting for transfers between devices  120 us (39%)
  matrix products  70.1 us (23%)
  local copies, waits for them, and re-layouts  44.6 us (14%)
  other arithmetic  29.8 us (10%)
  between operations  25.9 us (8%)
  starting transfers between devices  16 us (5%)
    all_gather x1, waiting for transfers between devices, on_device(): kv_all = lax.all_gather(kv, ('seq', 'tl'), axis=2, tiled=True)  58.3 us
    all_gather x1, waiting for transfers between devices, on_device(): lax.all_gather(jnp.where(core == 0, query_weight, jnp.concatenate([key_we...  47.1 us
    dot_general x6, matrix products, tile(): jnp.einsum('qkgd,ktd->kgqt', q_chunks[chunk], k_block, preferred_element_...  24.1 us
    dot_general x6, matrix products, tile(): jnp.einsum('kgqt,ktd->qkgd', weights.astype(jnp.bfloat16), v_block, prefe...  23.8 us
    unnamed x2, matrix products  11.9 us
    all_to_all x2, starting transfers between devices, attend(): lax.all_to_all(partial.reshape(n_group, member_part, -1), 'th', 0, 0, til...  10.6 us
    dot_general x2, matrix products, attend(): jnp.dot(attended, pair_out, preferred_element_type=jnp.float32)  10.3 us
    all_gather x1, waiting for transfers between devices, on_device(): pair_out = lax.all_gather(out_weight, 'tl', axis=0, tiled=True)  9.01 us
  transfers between devices with their start and end apart: 7, of which 4 were waited for; matrix products, arithmetic and copies ran while one was open for 39% of the time, Pallas kernels for 0%

profile of v4, /device:TPU:4, one launch (start us, length us, event | category | flops | bytes accessed | tf_op | source)
XLA Modules:
  0.0 307.0 jit_solution(17046801886150701751)
XLA Ops:
  16.7 5.1 %all-to-all-start = ((bf16[8,64,4608]{2,1,0:T(8,128)(2,1)}), bf16[8,64,4608]{2,1,0:T(8,128)(2,1)}, u32[]{:S(2)}, u32[]{:S(2)}) async-start(bf16[8,64,4608]{2,1,0:T(8,128)(2,1)} %broadcast_in_dim.133), calls=%async_computation | async-start | bytes 9437184 | tf_op jit(solution)/shard_map/all_to_all | solution.py:89
  21.9 47.1 %all-gather.9.cloned.1.call-done = bf16[18432,128]{1,0:T(8,128)(2,1)} async-done(((bf16[4608,128]{1,0:T(8,128)(2,1)}), bf16[18432,128]{1,0:T(8,128)(2,1)}) %all-gather.9.cloned.1.call-update) | async-done | bytes 4718608 | tf_op jit(solution)/shard_map/all_gather | solution.py:79
  69.0 6.8 %copy.82 = bf16[4,4608,128]{1,2,0:T(8,128)(2,1)} copy(bf16[4,4608,128]{2,1,0:T(8,128)(2,1)} %bitcast.173) | data formatting | bytes 9437184 | tf_op jit(solution)/shard_map/all_gather | solution.py:79
  83.3 5.9 %fusion.86 = f32[512,512]{0,1:S(1)} fusion(bf16[512,4608]{1,0:T(8,128)(2,1)} %bitcast.22, bf16[4608,512]{0,1:T(8,128)(2,1)} %bitcast.172), kind=kOutput, calls=%fused_computation.174 | convolution fusion | flops 2415919104 | bytes 10485760
  89.3 5.9 %fusion.87 = f32[512,512]{0,1:S(1)} fusion(bf16[512,4608]{1,0:T(8,128)(2,1)} %bitcast.22, bf16[4608,512]{0,1:T(8,128)(2,1)} %bitcast.28), kind=kOutput, calls=%fused_computation.175 | convolution fusion | flops 2415919104 | bytes 10485760
  110.3 58.3 %all-gather.5.cloned.1.call-done = bf16[2,2,8192,128]{3,2,1,0:T(8,128)(2,1)} async-done(((bf16[2,2,512,128]{3,2,1,0:T(8,128)(2,1)}), bf16[2,2,8192,128]{3,2,1,0:T(8,128)(2,1)}) %all-gather.5.cloned.1.call-update) | async-done | bytes 8388624 | tf_op jit(solution)/shard_map/all_gather | solution.py:119
  168.6 4.4 %fusion.84 = (bf16[1,2,4,8,4,64,128]{6,5,3,4,2,1,0:T(8,128)(2,1)S(1)}, bf16[1,2,4,8,4,64,128]{6,5,3,4,2,1,0:T(8,128)(2,1)S(1)}) fusion(bf16[2,2,4,8,4,64,128]{6,5,3,4,2,1,0:T(8,128)(2,1)} %bitcast.171), kind=kLoop, calls=%fused_computation.172 | loop fusion | bytes 16777216 | tf_op jit(solution)/shard_map/slice | solution.py:122
  178.9 6.5 %copy.95 = bf16[2,8192,128]{1,2,0:T(8,128)(2,1)} copy(bf16[2,8192,128]{2,1,0:T(8,128)(2,1)} %bitcast.166) | data formatting | bytes 8388608 | tf_op jit(solution)/shard_map/while | solution.py:176
  185.4 28.7 %while.28 = (s32[]{:T(128)}, f32[256,2,2,128]{0,3,2,1:T(8,128)S(1)}, f32[2,2,256]{2,1,0:T(2,128)S(1)}, s32[]{:T(128)}, bf16[2,8192,128]{1,2,0:T(8,128)(2,1)}, /*...) while((s32[]{:T(128)}, ...), condition=%wide.region_7.8_spmd, body=%wide.region_5.7_spmd.sunk | while | flops 1096419328 | bytes 21821636 | solution.py:176
  187.0 4.0 %fusion.106 = (f32[2,2,256]{2,1,0:T(2,128)S(1)}, f32[2,2048,256,2]{2,1,3,0:T(8,128)S(1)}) fusion(pred[256,2048]{0,1:T(8,128)(4,1)S(1)} %compare_and_fusion.4, bf16[2,256,2,2,128]{4,1,3,2,0:T(8,128)(2,1)S(1)} %get-tuple-element.642, bf16[2,8192,128]{2,1,0:T(8,128)(2,1)} %get-tuple-element.641, s32[]{:T(128)S(6)} %select_n.419), kind=kOutput, calls=%fused_computation.2.clone.1 | convolution fusion | flops 547355648 | bytes 10227716 | tf_op jit(solution)/shard_map/while/body/qkgd,ktd->kgqt/dot_general | solution.py:150
  196.5 4.0 %fusion.106 = (f32[2,2,256]{2,1,0:T(2,128)S(1)}, f32[2,2048,256,2]{2,1,3,0:T(8,128)S(1)}) fusion(pred[256,2048]{0,1:T(8,128)(4,1)S(1)} %compare_and_fusion.4, bf16[2,256,2,2,128]{4,1,3,2,0:T(8,128)(2,1)S(1)} %get-tuple-element.642, bf16[2,8192,128]{2,1,0:T(8,128)(2,1)} %get-tuple-element.641, s32[]{:T(128)S(6)} %select_n.419), kind=kOutput, calls=%fused_computation.2.clone.1 | convolution fusion | flops 547355648 | bytes 10227716 | tf_op jit(solution)/shard_map/while/body/qkgd,ktd->kgqt/dot_general | solution.py:150
  206.1 4.0 %fusion.106 = (f32[2,2,256]{2,1,0:T(2,128)S(1)}, f32[2,2048,256,2]{2,1,3,0:T(8,128)S(1)}) fusion(pred[256,2048]{0,1:T(8,128)(4,1)S(1)} %compare_and_fusion.4, bf16[2,256,2,2,128]{4,1,3,2,0:T(8,128)(2,1)S(1)} %get-tuple-element.642, bf16[2,8192,128]{2,1,0:T(8,128)(2,1)} %get-tuple-element.641, s32[]{:T(128)S(6)} %select_n.419), kind=kOutput, calls=%fused_computation.2.clone.1 | convolution fusion | flops 547355648 | bytes 10227716 | tf_op jit(solution)/shard_map/while/body/qkgd,ktd->kgqt/dot_general | solution.py:150
  214.2 9.0 %all-gather.7.cloned.1.call-done = bf16[512,4608]{1,0:T(8,128)(2,1)} async-done(((bf16[128,4608]{1,0:T(8,128)(2,1)}), bf16[512,4608]{1,0:T(8,128)(2,1)}) %all-gather.7.cloned.1.call-update) | async-done | bytes 4718608 | tf_op jit(solution)/shard_map/all_gather | solution.py:86
  223.2 5.2 %convolution_convert_fusion.1 = bf16[256,4608]{1,0:T(8,128)(2,1)} fusion(bf16[256,512]{0,1:T(8,128)(2,1)S(1)} %bitcast.179, bf16[512,4608]{1,0:T(8,128)(2,1)} %all-gather.7.cloned.1.call-done), kind=kOutput, calls=%fused_computation.46 | convolution fusion | flops 1209139200 | bytes 7340032 | tf_op jit(solution)/shard_map/dot_general | solution.py:181
  228.4 4.9 %all-to-all-start.1 = ((bf16[8,32,4608]{2,1,0:T(8,128)(2,1)}), bf16[8,32,4608]{2,1,0:T(8,128)(2,1)S(1)}, u32[]{:S(2)}, u32[]{:S(2)}) async-start(bf16[8,32,4608]{2,1,0:T(8,128)(2,1)} %bitcast.170), calls=%async_computation.1 | async-start | bytes 4718592 | tf_op jit(solution)/shard_map/all_to_all | solution.py:184
  233.3 28.8 %while.29 = (s32[]{:T(128)}, f32[256,2,2,128]{0,3,2,1:T(8,128)S(1)}, f32[2,2,256]{2,1,0:T(2,128)S(1)}, s32[]{:T(128)}, bf16[2,8192,128]{1,2,0:T(8,128)(2,1)}, /*...) while((s32[]{:T(128)}, ...), condition=%wide.region_13.14_spmd, body=%wide.region_11.13_spmd.sunk | while | flops 1096419328 | bytes 21821636 | solution.py:176
  235.1 4.0 %fusion.110 = (f32[2,2,256]{2,1,0:T(2,128)S(1)}, f32[2,2048,256,2]{2,1,3,0:T(8,128)S(1)}) fusion(pred[256,2048]{0,1:T(8,128)(4,1)S(1)} %compare_and_fusion.5, bf16[2,256,2,2,128]{4,1,3,2,0:T(8,128)(2,1)S(1)} %get-tuple-element.600, bf16[2,8192,128]{2,1,0:T(8,128)(2,1)} %get-tuple-element.599, s32[]{:T(128)S(6)} %select_n.422), kind=kOutput, calls=%fused_computation.24.clone.1 | convolution fusion | flops 547355648 | bytes 10227716 | tf_op jit(solution)/shard_map/while/body/qkgd,ktd->kgqt/dot_general | solution.py:150
  244.6 4.0 %fusion.110 = (f32[2,2,256]{2,1,0:T(2,128)S(1)}, f32[2,2048,256,2]{2,1,3,0:T(8,128)S(1)}) fusion(pred[256,2048]{0,1:T(8,128)(4,1)S(1)} %compare_and_fusion.5, bf16[2,256,2,2,128]{4,1,3,2,0:T(8,128)(2,1)S(1)} %get-tuple-element.600, bf16[2,8192,128]{2,1,0:T(8,128)(2,1)} %get-tuple-element.599, s32[]{:T(128)S(6)} %select_n.422), kind=kOutput, calls=%fused_computation.24.clone.1 | convolution fusion | flops 547355648 | bytes 10227716 | tf_op jit(solution)/shard_map/while/body/qkgd,ktd->kgqt/dot_general | solution.py:150
  248.6 4.0 %fusion.111 = f32[256,2,2,128]{0,3,2,1:T(8,128)S(1)} fusion(f32[256,2,2,128]{0,3,2,1:T(8,128)S(1)} %get-tuple-element.578, f32[2,2048,256,2]{2,1,3,0:T(8,128)S(1)} %get-tuple-element.561, pred[256,2048]{0,1:T(8,128)(4,1)S(1)} %compare_and_fusion.5, bf16[2,8192,128]{1,2,0:T(8,128)(2,1)} %get-tuple-element.595, s32[]{:T(128)S(6)} %select_n.422), kind=kOutput, calls=%fused_computation.30.clone.1 | convolution fusion | flops 547487744 | bytes 11010052 | tf_op jit(solution)/shard_map/while/body/kgqt,ktd->qkgd/dot_general | solution.py:164
  254.1 4.0 %fusion.110 = (f32[2,2,256]{2,1,0:T(2,128)S(1)}, f32[2,2048,256,2]{2,1,3,0:T(8,128)S(1)}) fusion(pred[256,2048]{0,1:T(8,128)(4,1)S(1)} %compare_and_fusion.5, bf16[2,256,2,2,128]{4,1,3,2,0:T(8,128)(2,1)S(1)} %get-tuple-element.600, bf16[2,8192,128]{2,1,0:T(8,128)(2,1)} %get-tuple-element.599, s32[]{:T(128)S(6)} %select_n.422), kind=kOutput, calls=%fused_computation.24.clone.1 | convolution fusion | flops 547355648 | bytes 10227716 | tf_op jit(solution)/shard_map/while/body/qkgd,ktd->kgqt/dot_general | solution.py:150
  262.2 5.1 %convolution_convert_fusion = bf16[256,4608]{1,0:T(8,128)(2,1)} fusion(bf16[256,512]{0,1:T(8,128)(2,1)S(1)} %bitcast.180, bf16[512,4608]{1,0:T(8,128)(2,1)} %all-gather.7.cloned.1.call-done), kind=kOutput, calls=%fused_computation.45 | convolution fusion | flops 1209139200 | bytes 7340032 | tf_op jit(solution)/shard_map/dot_general | solution.py:181
  267.3 5.7 %all-to-all-start.2 = ((bf16[8,32,4608]{2,1,0:T(8,128)(2,1)}), bf16[8,32,4608]{2,1,0:T(8,128)(2,1)}, u32[]{:S(2)}, u32[]{:S(2)}) async-start(bf16[8,32,4608]{2,1,0:T(8,128)(2,1)} %bitcast.169), calls=%async_computation.2 | async-start | bytes 4718592 | tf_op jit(solution)/shard_map/all_to_all | solution.py:184
  276.9 5.3 %constant_dynamic-slice_fusion = (bf16[1,8192,64]{2,1,0:T(8,128)(2,1)}, bf16[1,8192,64]{2,1,0:T(8,128)(2,1)}) fusion(bf16[2,8192,128]{2,1,0:T(8,128)(2,1)} %bitcast.167, s32[]{:T(128)S(6)} %select_n.271, s32[]{:T(128)S(6)} %select_n.274, bf16[2,8192,128]{2,1,0:T(8,128)(2,1)} %get-tuple-element.656), kind=kLoop, calls=%fused_computation.151 | loop fusion | bytes 4194312 | tf_op jit(solution)/shard_map/dynamic_slice | solution.py:201
  291.1 5.1 %all-to-all-done.2 = bf16[8,32,4608]{2,1,0:T(8,128)(2,1)} async-done(((bf16[8,32,4608]{2,1,0:T(8,128)(2,1)}), bf16[8,32,4608]{2,1,0:T(8,128)(2,1)}, u32[]{:S(2)}, u32[]{:S(2)}) %all-to-all-start.2) | async-done | bytes 2359328 | tf_op jit(solution)/shard_map/all_to_all | solution.py:184
  (132 shorter events, 72.0 us)
Async XLA Ops:
  7.2 61.8 %all-gather.9.cloned.1.call-start = ((), (), s32[]{:S(2)}) async-start(), calls=%async_computation.5 | async-start | bytes 5898240 | tf_op jit(solution)/shard_map/all_gather | solution.py:79
  8.9 4.8 %copy-start.1 = (bf16[64,4608]{1,0:T(8,128)(2,1)S(1)}, bf16[64,4608]{1,0:T(8,128)(2,1)}, u32[]{:S(2)}) copy-start(bf16[64,4608]{1,0:T(8,128)(2,1)} %param.14) | copy-start | bytes 1769476
  8.9 5.1 %copy-start.4 = (f32[4608]{0:T(1024)S(1)}, f32[4608]{0:T(1024)}, u32[]{:S(2)}) copy-start(f32[4608]{0:T(1024)} %param.15) | copy-start | bytes 55300
  16.7 66.6 %all-to-all-start = ((bf16[8,64,4608]{2,1,0:T(8,128)(2,1)}), bf16[8,64,4608]{2,1,0:T(8,128)(2,1)}, u32[]{:S(2)}, u32[]{:S(2)}) async-start(bf16[8,64,4608]{2,1,0:T(8,128)(2,1)} %broadcast_in_dim.133), calls=%async_computation | async-start | bytes 9437184 | tf_op jit(solution)/shard_map/all_to_all | solution.py:89
  21.8 146.8 %all-gather.5.cloned.1.call-start = ((), (), s32[]{:S(2)}) async-start(), calls=%async_computation.3 | async-start | bytes 8912896 | tf_op jit(solution)/shard_map/all_gather | solution.py:119
  69.0 6.8 %copy-start.6 = (s32[3]{0:T(128)S(1)}, s32[3]{0:T(128)}, u32[]{:S(2)}) copy-start(s32[3]{0:T(128)} %param.21) | copy-start | bytes 40
  69.0 7.0 %copy-start = (s32[8192]{0:T(1024)S(1)}, s32[8192]{0:T(1024)}, u32[]{:S(2)}) copy-start(s32[8192]{0:T(1024)} %param.22) | copy-start | bytes 98308
  69.0 10.2 %copy-start.7 = (s32[3]{0:T(128)S(1)}, s32[3]{0:T(128)}, u32[]{:S(2)}) copy-start(s32[3]{0:T(128)} %param.23) | copy-start | bytes 40
  75.8 13.5 %collective-permute-start = (bf16[4,4608,128]{1,2,0:T(8,128)(2,1)}, bf16[4,4608,128]{1,2,0:T(8,128)(2,1)}, u32[]{:S(2)}, u32[]{:S(2)}) collective-permute-start(bf16[4,4608,128]{1,2,0:T(8,128)(2,1)} %copy.82), channel_id=1, source_target_pairs={{0,32},{32,0},{64,96},{96,64},{1,33},{33,1},{65,97},{97,65},{2,34}... | collective-permute-start | bytes 14155784 | tf_op jit(solution)/shard_map/ppermute | solution.py:85
  97.6 125.6 %all-gather.7.cloned.1.call-start = ((), (), s32[]{:S(2)}) async-start(), calls=%async_computation.4 | async-start | bytes 5898240 | tf_op jit(solution)/shard_map/all_gather | solution.py:86
  228.4 38.9 %all-to-all-start.1 = ((bf16[8,32,4608]{2,1,0:T(8,128)(2,1)}), bf16[8,32,4608]{2,1,0:T(8,128)(2,1)S(1)}, u32[]{:S(2)}, u32[]{:S(2)}) async-start(bf16[8,32,4608]{2,1,0:T(8,128)(2,1)} %bitcast.170), calls=%async_computation.1 | async-start | bytes 4718592 | tf_op jit(solution)/shard_map/all_to_all | solution.py:184
  267.3 28.8 %all-to-all-start.2 = ((bf16[8,32,4608]{2,1,0:T(8,128)(2,1)}), bf16[8,32,4608]{2,1,0:T(8,128)(2,1)}, u32[]{:S(2)}, u32[]{:S(2)}) async-start(bf16[8,32,4608]{2,1,0:T(8,128)(2,1)} %bitcast.169), calls=%async_computation.2 | async-start | bytes 4718592 | tf_op jit(solution)/shard_map/all_to_all | solution.py:184
  288.3 11.1 %copy-start.2 = (bf16[64,4608]{1,0:T(8,128)(2,1)S(1)}, bf16[64,4608]{1,0:T(8,128)(2,1)}, u32[]{:S(2)}) copy-start(bf16[64,4608]{1,0:T(8,128)(2,1)} %param.14) | copy-start | bytes 1769476
  288.3 11.1 %copy-start.5 = (f32[4608]{0:T(1024)S(1)}, f32[4608]{0:T(1024)}, u32[]{:S(2)}) copy-start(f32[4608]{0:T(1024)} %param.20) | copy-start | bytes 55300
  291.0 8.4 %copy-start.3 = (f32[32,4608]{1,0:T(8,128)S(1)}, f32[32,4608]{1,0:T(8,128)}, u32[]{:S(2)}) copy-start(f32[32,4608]{1,0:T(8,128)} %convert_reduce_fusion.1) | copy-start | bytes 1769476
Sparse Core Ops, SparseCore 0:
  13.8 55.1 all-gather.8
  97.7 70.8 all-gather.4
  170.3 52.8 all-gather.6

commit v5 on v3

--- a/solution.py
+++ b/solution.py
@@ -14,7 +14,7 @@
 SCORE_SHIFT = 20.0
 ROPE_BASE = 10000.0
 KEY_TILE = 1024
-Q_CHUNKS = 2
+Q_CHUNKS = 1
 HEADS_PER_DEVICE = 4
 
 

time: 311 us -> 304 us (0.977); the launches traced: 306 us -> 302 us
  matrix products: 53.1 us -> 66.7 us
  local copies, waits for them, and re-layouts: 46.2 us -> 35.8 us
  between operations: 25.8 us -> 20.9 us
  starting transfers between devices: 14.7 us -> 11 us
    all_gather x1, waiting for transfers between devices: 20.2 us -> 0.02 us  [on_device(): pair_out = lax.all_gather(out_weight, 'tl', axis=0, tiled=True)]
    all_to_all x2 -> x1, waiting for transfers between devices: 16.2 us -> 29.2 us  [attend(): lax.all_to_all(partial.reshape(n_group, member_part, -1), 'th', 0, 0, til...]
    dot_general x6, matrix products: 15.3 us -> 25.1 us  [tile(): jnp.einsum('qkgd,ktd->kgqt', q_chunks[chunk], k_block, preferred_element_...]
    dot_general x6, matrix products: 15.6 us -> 23.1 us  [tile(): jnp.einsum('kgqt,ktd->qkgd', weights.astype(jnp.bfloat16), v_block, prefe...]
    all_gather x1, waiting for transfers between devices: 58.3 us -> 65 us  [on_device(): kv_all = lax.all_gather(kv, ('seq', 'tl'), axis=2, tiled=True)]
    while x1 -> x0, local copies, waits for them, and re-layouts: 6.53 us -> none  [attend(): lax.fori_loop(lo_tile, hi_tile, tile, (zero_numer, zero_denom))]
    dynamic_slice x2, local copies, waits for them, and re-layouts: 8.05 us -> 3.84 us  [on_device(): lax.dynamic_slice_in_dim(lax.dynamic_index_in_dim(value_rows, own_head, 0...]
    dot_general x2 -> x1, matrix products: 10.3 us -> 6.6 us  [attend(): jnp.dot(attended, pair_out, preferred_element_type=jnp.float32)]
  transfers between devices with their start and end apart: 7 -> 6, of which waited for: 5 -> 3; matrix products, arithmetic and copies ran while one was open for 32% -> 33% of each run, Pallas kernels for 0% -> 0%
where the time goes in v5:
time: 304 us; the launch traced here: 302 us
  waiting for transfers between devices  142 us (47%)
  matrix products  66.7 us (22%)
  local copies, waits for them, and re-layouts  35.8 us (12%)
  other arithmetic  25.4 us (8%)
  between operations  20.9 us (7%)
  starting transfers between devices  11 us (4%)
    all_gather x1, waiting for transfers between devices, on_device(): kv_all = lax.all_gather(kv, ('seq', 'tl'), axis=2, tiled=True)  65 us
    all_gather x1, waiting for transfers between devices, on_device(): lax.all_gather(jnp.where(core == 0, query_weight, jnp.concatenate([key_we...  47.1 us
    all_to_all x1, waiting for transfers between devices, attend(): lax.all_to_all(partial.reshape(n_group, member_part, -1), 'th', 0, 0, til...  29.2 us
    dot_general x6, matrix products, tile(): jnp.einsum('qkgd,ktd->kgqt', q_chunks[chunk], k_block, preferred_element_...  25.1 us
    dot_general x6, matrix products, tile(): jnp.einsum('kgqt,ktd->qkgd', weights.astype(jnp.bfloat16), v_block, prefe...  23.1 us
    unnamed x2, matrix products  11.9 us
    slice x2, local copies, waits for them, and re-layouts, on_device(): key_rows = kv_all[0]  7.37 us
    all_gather x1, local copies, waits for them, and re-layouts, on_device(): lax.all_gather(jnp.where(core == 0, query_weight, jnp.concatenate([key_we...  6.81 us
  transfers between devices with their start and end apart: 6, of which 3 were waited for; matrix products, arithmetic and copies ran while one was open for 33% of the time, Pallas kernels for 0%

profile of v5, /device:TPU:4, one launch (start us, length us, event | category | flops | bytes accessed | tf_op | source)
XLA Modules:
  0.0 302.4 jit_solution(201033158327310555)
XLA Ops:
  11.2 3.4 %maximum_select_fusion.1 = bf16[4608,128]{1,0:T(8,128)(2,1)} fusion(bf16[4608,128]{1,0:T(8,128)(2,1)} %param.14, bf16[4608,64]{1,0:T(8,128)(2,1)S(1)} %copy.66, bf16[4608,64]{1,0:T(8,128)(2,1)} %copy.65, pred[]{:T(512)S(6)} %eq.90), kind=kLoop, calls=%fused_computation.54 | loop fusion | flops 2949120 | bytes 3538945 | tf_op jit(solution)/shard_map/jit(_where)/select_n | solution.py:80
  17.7 5.1 %all-to-all-start = ((bf16[8,64,4608]{2,1,0:T(8,128)(2,1)}), bf16[8,64,4608]{2,1,0:T(8,128)(2,1)}, u32[]{:S(2)}, u32[]{:S(2)}) async-start(bf16[8,64,4608]{2,1,0:T(8,128)(2,1)} %broadcast_in_dim.120), calls=%async_computation | async-start | bytes 9437184 | tf_op jit(solution)/shard_map/all_to_all | solution.py:89
  22.8 47.1 %all-gather.9.cloned.1.call-done = bf16[18432,128]{1,0:T(8,128)(2,1)} async-done(((bf16[4608,128]{1,0:T(8,128)(2,1)}), bf16[18432,128]{1,0:T(8,128)(2,1)}) %all-gather.9.cloned.1.call-update) | async-done | bytes 4718608 | tf_op jit(solution)/shard_map/all_gather | solution.py:79
  69.9 6.8 %copy.67 = bf16[4,4608,128]{1,2,0:T(8,128)(2,1)} copy(bf16[4,4608,128]{2,1,0:T(8,128)(2,1)} %bitcast.101) | data formatting | bytes 9437184 | tf_op jit(solution)/shard_map/all_gather | solution.py:79
  85.1 5.9 %fusion.69 = f32[512,512]{0,1:S(1)} fusion(bf16[512,4608]{1,0:T(8,128)(2,1)} %bitcast.3, bf16[4608,512]{0,1:T(8,128)(2,1)} %bitcast.100), kind=kOutput, calls=%fused_computation.135 | convolution fusion | flops 2415919104 | bytes 10485760
  91.0 5.9 %fusion.70 = f32[512,512]{0,1:S(1)} fusion(bf16[512,4608]{1,0:T(8,128)(2,1)} %bitcast.3, bf16[4608,512]{0,1:T(8,128)(2,1)} %bitcast.9), kind=kOutput, calls=%fused_computation.136 | convolution fusion | flops 2415919104 | bytes 10485760
  105.3 65.0 %all-gather.5.cloned.1.call-done = bf16[2,2,8192,128]{3,2,1,0:T(8,128)(2,1)} async-done(((bf16[2,2,512,128]{3,2,1,0:T(8,128)(2,1)}), bf16[2,2,8192,128]{3,2,1,0:T(8,128)(2,1)}) %all-gather.5.cloned.1.call-update) | async-done | bytes 8388624 | tf_op jit(solution)/shard_map/all_gather | solution.py:119
  170.3 4.4 %fusion.67 = (bf16[1,2,4,8,4,64,128]{6,5,3,4,2,1,0:T(8,128)(2,1)S(1)}, bf16[1,2,4,8,4,64,128]{6,5,3,4,2,1,0:T(8,128)(2,1)S(1)}) fusion(bf16[2,2,4,8,4,64,128]{6,5,3,4,2,1,0:T(8,128)(2,1)} %bitcast.99), kind=kLoop, calls=%fused_computation.133 | loop fusion | bytes 16777216 | tf_op jit(solution)/shard_map/slice | solution.py:122
  180.8 54.1 %while.15 = (s32[]{:T(128)}, f32[512,2,2,128]{0,3,2,1:T(8,128)S(1)}, f32[2,2,512]{2,1,0:T(2,128)S(1)}, s32[]{:T(128)}, bf16[2,8192,128]{2,1,0:T(8,128)(2,1)}, /*...) while((s32[]{:T(128)}, ...), condition=%wide.region_7.8_spmd.clone, body=%wide.region_5.7_spmd.clone.sunk | while | flops 1096558080 | bytes 22079708 | solution.py:176
  181.9 4.2 %fusion.88 = (f32[2,2,512]{2,1,0:T(2,128)S(1)}, f32[2,1024,512,2]{2,1,3,0:T(8,128)S(1)}) fusion(pred[512,1024]{0,1:T(8,128)(4,1)S(1)} %compare_and_fusion.2, bf16[512,2,2,128]{3,0,2,1:T(8,128)(2,1)S(1)} %bitcast.110, bf16[2,8192,128]{2,1,0:T(8,128)(2,1)} %get-tuple-element.383, s32[]{:T(128)S(6)} %select_n.348), kind=kOutput, calls=%fused_computation.3.clone.1 | convolution fusion | flops 547354624 | bytes 9969668 | tf_op jit(solution)/shard_map/while/body/qkgd,ktd->kgqt/dot_general | solution.py:150
  186.1 3.8 %fusion.89 = f32[512,2,2,128]{0,3,2,1:T(8,128)S(1)} fusion(f32[512,2,2,128]{0,3,2,1:T(8,128)S(1)} %get-tuple-element.362, f32[2,1024,512,2]{2,1,3,0:T(8,128)S(1)} %get-tuple-element.344, pred[512,1024]{0,1:T(8,128)(4,1)S(1)} %compare_and_fusion.2, bf16[2,8192,128]{2,1,0:T(8,128)(2,1)} %get-tuple-element.380, s32[]{:T(128)S(6)} %select_n.348), kind=kOutput, calls=%fused_computation.9.clone.1 | convolution fusion | flops 547618816 | bytes 11534340 | tf_op jit(solution)/shard_map/while/body/kgqt,ktd->qkgd/dot_general | solution.py:164
  190.9 4.2 %fusion.88 = (f32[2,2,512]{2,1,0:T(2,128)S(1)}, f32[2,1024,512,2]{2,1,3,0:T(8,128)S(1)}) fusion(pred[512,1024]{0,1:T(8,128)(4,1)S(1)} %compare_and_fusion.2, bf16[512,2,2,128]{3,0,2,1:T(8,128)(2,1)S(1)} %bitcast.110, bf16[2,8192,128]{2,1,0:T(8,128)(2,1)} %get-tuple-element.383, s32[]{:T(128)S(6)} %select_n.348), kind=kOutput, calls=%fused_computation.3.clone.1 | convolution fusion | flops 547354624 | bytes 9969668 | tf_op jit(solution)/shard_map/while/body/qkgd,ktd->kgqt/dot_general | solution.py:150
  195.1 3.9 %fusion.89 = f32[512,2,2,128]{0,3,2,1:T(8,128)S(1)} fusion(f32[512,2,2,128]{0,3,2,1:T(8,128)S(1)} %get-tuple-element.362, f32[2,1024,512,2]{2,1,3,0:T(8,128)S(1)} %get-tuple-element.344, pred[512,1024]{0,1:T(8,128)(4,1)S(1)} %compare_and_fusion.2, bf16[2,8192,128]{2,1,0:T(8,128)(2,1)} %get-tuple-element.380, s32[]{:T(128)S(6)} %select_n.348), kind=kOutput, calls=%fused_computation.9.clone.1 | convolution fusion | flops 547618816 | bytes 11534340 | tf_op jit(solution)/shard_map/while/body/kgqt,ktd->qkgd/dot_general | solution.py:164
  199.9 4.2 %fusion.88 = (f32[2,2,512]{2,1,0:T(2,128)S(1)}, f32[2,1024,512,2]{2,1,3,0:T(8,128)S(1)}) fusion(pred[512,1024]{0,1:T(8,128)(4,1)S(1)} %compare_and_fusion.2, bf16[512,2,2,128]{3,0,2,1:T(8,128)(2,1)S(1)} %bitcast.110, bf16[2,8192,128]{2,1,0:T(8,128)(2,1)} %get-tuple-element.383, s32[]{:T(128)S(6)} %select_n.348), kind=kOutput, calls=%fused_computation.3.clone.1 | convolution fusion | flops 547354624 | bytes 9969668 | tf_op jit(solution)/shard_map/while/body/qkgd,ktd->kgqt/dot_general | solution.py:150
  204.1 3.9 %fusion.89 = f32[512,2,2,128]{0,3,2,1:T(8,128)S(1)} fusion(f32[512,2,2,128]{0,3,2,1:T(8,128)S(1)} %get-tuple-element.362, f32[2,1024,512,2]{2,1,3,0:T(8,128)S(1)} %get-tuple-element.344, pred[512,1024]{0,1:T(8,128)(4,1)S(1)} %compare_and_fusion.2, bf16[2,8192,128]{2,1,0:T(8,128)(2,1)} %get-tuple-element.380, s32[]{:T(128)S(6)} %select_n.348), kind=kOutput, calls=%fused_computation.9.clone.1 | convolution fusion | flops 547618816 | bytes 11534340 | tf_op jit(solution)/shard_map/while/body/kgqt,ktd->qkgd/dot_general | solution.py:164
  208.9 4.2 %fusion.88 = (f32[2,2,512]{2,1,0:T(2,128)S(1)}, f32[2,1024,512,2]{2,1,3,0:T(8,128)S(1)}) fusion(pred[512,1024]{0,1:T(8,128)(4,1)S(1)} %compare_and_fusion.2, bf16[512,2,2,128]{3,0,2,1:T(8,128)(2,1)S(1)} %bitcast.110, bf16[2,8192,128]{2,1,0:T(8,128)(2,1)} %get-tuple-element.383, s32[]{:T(128)S(6)} %select_n.348), kind=kOutput, calls=%fused_computation.3.clone.1 | convolution fusion | flops 547354624 | bytes 9969668 | tf_op jit(solution)/shard_map/while/body/qkgd,ktd->kgqt/dot_general | solution.py:150
  213.1 3.8 %fusion.89 = f32[512,2,2,128]{0,3,2,1:T(8,128)S(1)} fusion(f32[512,2,2,128]{0,3,2,1:T(8,128)S(1)} %get-tuple-element.362, f32[2,1024,512,2]{2,1,3,0:T(8,128)S(1)} %get-tuple-element.344, pred[512,1024]{0,1:T(8,128)(4,1)S(1)} %compare_and_fusion.2, bf16[2,8192,128]{2,1,0:T(8,128)(2,1)} %get-tuple-element.380, s32[]{:T(128)S(6)} %select_n.348), kind=kOutput, calls=%fused_computation.9.clone.1 | convolution fusion | flops 547618816 | bytes 11534340 | tf_op jit(solution)/shard_map/while/body/kgqt,ktd->qkgd/dot_general | solution.py:164
  217.8 4.2 %fusion.88 = (f32[2,2,512]{2,1,0:T(2,128)S(1)}, f32[2,1024,512,2]{2,1,3,0:T(8,128)S(1)}) fusion(pred[512,1024]{0,1:T(8,128)(4,1)S(1)} %compare_and_fusion.2, bf16[512,2,2,128]{3,0,2,1:T(8,128)(2,1)S(1)} %bitcast.110, bf16[2,8192,128]{2,1,0:T(8,128)(2,1)} %get-tuple-element.383, s32[]{:T(128)S(6)} %select_n.348), kind=kOutput, calls=%fused_computation.3.clone.1 | convolution fusion | flops 547354624 | bytes 9969668 | tf_op jit(solution)/shard_map/while/body/qkgd,ktd->kgqt/dot_general | solution.py:150
  222.0 3.8 %fusion.89 = f32[512,2,2,128]{0,3,2,1:T(8,128)S(1)} fusion(f32[512,2,2,128]{0,3,2,1:T(8,128)S(1)} %get-tuple-element.362, f32[2,1024,512,2]{2,1,3,0:T(8,128)S(1)} %get-tuple-element.344, pred[512,1024]{0,1:T(8,128)(4,1)S(1)} %compare_and_fusion.2, bf16[2,8192,128]{2,1,0:T(8,128)(2,1)} %get-tuple-element.380, s32[]{:T(128)S(6)} %select_n.348), kind=kOutput, calls=%fused_computation.9.clone.1 | convolution fusion | flops 547618816 | bytes 11534340 | tf_op jit(solution)/shard_map/while/body/kgqt,ktd->qkgd/dot_general | solution.py:164
  226.8 4.2 %fusion.88 = (f32[2,2,512]{2,1,0:T(2,128)S(1)}, f32[2,1024,512,2]{2,1,3,0:T(8,128)S(1)}) fusion(pred[512,1024]{0,1:T(8,128)(4,1)S(1)} %compare_and_fusion.2, bf16[512,2,2,128]{3,0,2,1:T(8,128)(2,1)S(1)} %bitcast.110, bf16[2,8192,128]{2,1,0:T(8,128)(2,1)} %get-tuple-element.383, s32[]{:T(128)S(6)} %select_n.348), kind=kOutput, calls=%fused_computation.3.clone.1 | convolution fusion | flops 547354624 | bytes 9969668 | tf_op jit(solution)/shard_map/while/body/qkgd,ktd->kgqt/dot_general | solution.py:150
  231.0 3.8 %fusion.89 = f32[512,2,2,128]{0,3,2,1:T(8,128)S(1)} fusion(f32[512,2,2,128]{0,3,2,1:T(8,128)S(1)} %get-tuple-element.362, f32[2,1024,512,2]{2,1,3,0:T(8,128)S(1)} %get-tuple-element.344, pred[512,1024]{0,1:T(8,128)(4,1)S(1)} %compare_and_fusion.2, bf16[2,8192,128]{2,1,0:T(8,128)(2,1)} %get-tuple-element.380, s32[]{:T(128)S(6)} %select_n.348), kind=kOutput, calls=%fused_computation.9.clone.1 | convolution fusion | flops 547618816 | bytes 11534340 | tf_op jit(solution)/shard_map/while/body/kgqt,ktd->qkgd/dot_general | solution.py:164
  235.1 6.6 %convolution_convert_fusion = bf16[512,4608]{1,0:T(8,128)(2,1)} fusion(bf16[512,512]{0,1:T(8,128)(2,1)S(1)} %bitcast.104, bf16[512,4608]{1,0:T(8,128)(2,1)} %all-gather.7.cloned.1.call-done), kind=kOutput, calls=%fused_computation.39 | convolution fusion | flops 2418278400 | bytes 9961472 | tf_op jit(solution)/shard_map/dot_general | solution.py:181
  241.7 5.8 %all-to-all-start.1 = ((bf16[8,64,4608]{2,1,0:T(8,128)(2,1)}), bf16[8,64,4608]{2,1,0:T(8,128)(2,1)}, u32[]{:S(2)}, u32[]{:S(2)}) async-start(bf16[8,64,4608]{2,1,0:T(8,128)(2,1)} %bitcast.96), calls=%async_computation.1 | async-start | bytes 9437184 | tf_op jit(solution)/shard_map/all_to_all | solution.py:184
  262.3 29.2 %all-to-all-done.1 = bf16[8,64,4608]{2,1,0:T(8,128)(2,1)} async-done(((bf16[8,64,4608]{2,1,0:T(8,128)(2,1)}), bf16[8,64,4608]{2,1,0:T(8,128)(2,1)}, u32[]{:S(2)}, u32[]{:S(2)}) %all-to-all-start.1) | async-done | bytes 4718624 | tf_op jit(solution)/shard_map/all_to_all | solution.py:184
  (100 shorter events, 47.4 us)
Async XLA Ops:
  7.2 62.8 %all-gather.9.cloned.1.call-start = ((), (), s32[]{:S(2)}) async-start(), calls=%async_computation.4 | async-start | bytes 5898240 | tf_op jit(solution)/shard_map/all_gather | solution.py:79
  8.9 5.8 %copy-start.1 = (bf16[64,4608]{1,0:T(8,128)(2,1)S(1)}, bf16[64,4608]{1,0:T(8,128)(2,1)}, u32[]{:S(2)}) copy-start(bf16[64,4608]{1,0:T(8,128)(2,1)} %param.12) | copy-start | bytes 1769476
  8.9 6.0 %copy-start.2 = (f32[4608]{0:T(1024)S(1)}, f32[4608]{0:T(1024)}, u32[]{:S(2)}) copy-start(f32[4608]{0:T(1024)} %param.13) | copy-start | bytes 55300
  17.7 67.4 %all-to-all-start = ((bf16[8,64,4608]{2,1,0:T(8,128)(2,1)}), bf16[8,64,4608]{2,1,0:T(8,128)(2,1)}, u32[]{:S(2)}, u32[]{:S(2)}) async-start(bf16[8,64,4608]{2,1,0:T(8,128)(2,1)} %broadcast_in_dim.120), calls=%async_computation | async-start | bytes 9437184 | tf_op jit(solution)/shard_map/all_to_all | solution.py:89
  22.8 147.6 %all-gather.5.cloned.1.call-start = ((), (), s32[]{:S(2)}) async-start(), calls=%async_computation.2 | async-start | bytes 8912896 | tf_op jit(solution)/shard_map/all_gather | solution.py:119
  69.9 6.8 %copy-start.4 = (s32[3]{0:T(128)S(1)}, s32[3]{0:T(128)}, u32[]{:S(2)}) copy-start(s32[3]{0:T(128)} %param.19) | copy-start | bytes 40
  69.9 7.0 %copy-start = (s32[8192]{0:T(1024)S(1)}, s32[8192]{0:T(1024)}, u32[]{:S(2)}) copy-start(s32[8192]{0:T(1024)} %param.20) | copy-start | bytes 98308
  69.9 10.2 %copy-start.5 = (s32[3]{0:T(128)S(1)}, s32[3]{0:T(128)}, u32[]{:S(2)}) copy-start(s32[3]{0:T(128)} %param.21) | copy-start | bytes 40
  76.8 14.3 %collective-permute-start = (bf16[4,4608,128]{1,2,0:T(8,128)(2,1)}, bf16[4,4608,128]{1,2,0:T(8,128)(2,1)}, u32[]{:S(2)}, u32[]{:S(2)}) collective-permute-start(bf16[4,4608,128]{1,2,0:T(8,128)(2,1)} %copy.67), channel_id=1, source_target_pairs={{0,32},{32,0},{64,96},{96,64},{1,33},{33,1},{65,97},{97,65},{2,34}... | collective-permute-start | bytes 14155784 | tf_op jit(solution)/shard_map/ppermute | solution.py:85
  99.4 135.7 %all-gather.7.cloned.1.call-start = ((), (), s32[]{:S(2)}) async-start(), calls=%async_computation.3 | async-start | bytes 5898240 | tf_op jit(solution)/shard_map/all_gather | solution.py:86
  241.7 49.8 %all-to-all-start.1 = ((bf16[8,64,4608]{2,1,0:T(8,128)(2,1)}), bf16[8,64,4608]{2,1,0:T(8,128)(2,1)}, u32[]{:S(2)}, u32[]{:S(2)}) async-start(bf16[8,64,4608]{2,1,0:T(8,128)(2,1)} %bitcast.96), calls=%async_computation.1 | async-start | bytes 9437184 | tf_op jit(solution)/shard_map/all_to_all | solution.py:184
  260.7 34.1 %copy-start.3 = (f32[4608]{0:T(1024)S(1)}, f32[4608]{0:T(1024)}, u32[]{:S(2)}) copy-start(f32[4608]{0:T(1024)} %param.18) | copy-start | bytes 55300
Sparse Core Ops, SparseCore 0:
  14.8 55.1 all-gather.8
  99.5 70.8 all-gather.4
  172.0 52.8 all-gather.6

commit v6 on v5

--- a/solution.py
+++ b/solution.py
@@ -13,7 +13,7 @@
 QUERY_SCALE = 144.0 ** (-0.5)
 SCORE_SHIFT = 20.0
 ROPE_BASE = 10000.0
-KEY_TILE = 1024
+KEY_TILE = 2048
 Q_CHUNKS = 1
 HEADS_PER_DEVICE = 4
 

time: 304 us -> 303 us (level)
  waiting for transfers between devices: 142 us -> 149 us
  matrix products: 66.7 us -> 60.9 us
    all_to_all x1, waiting for transfers between devices: 29.2 us -> 36.5 us  [attend(): lax.all_to_all(partial.reshape(n_group, member_part, -1), 'th', 0, 0, til...]
    dot_general x6 -> x3, matrix products: 23.1 us -> 19.8 us  [tile(): jnp.einsum('kgqt,ktd->qkgd', weights.astype(jnp.bfloat16), v_block, prefe...]
    dot_general x6 -> x3, matrix products: 25.1 us -> 22.6 us  [tile(): jnp.einsum('qkgd,ktd->kgqt', q_chunks[chunk], k_block, preferred_element_...]
  transfers between devices with their start and end apart: 6 -> 6, of which waited for: 3 -> 3; matrix products, arithmetic and copies ran while one was open for 33% -> 31% of each run, Pallas kernels for 0% -> 0%
where the time goes in v6:
time: 303 us; the launch traced here: 301 us
  waiting for transfers between devices  149 us (49%)
  matrix products  60.9 us (20%)
  local copies, waits for them, and re-layouts  34.3 us (11%)
  other arithmetic  24.4 us (8%)
  between operations  20.9 us (7%)
  starting transfers between devices  11.1 us (4%)
    all_gather x1, waiting for transfers between devices, on_device(): kv_all = lax.all_gather(kv, ('seq', 'tl'), axis=2, tiled=True)  65 us
    all_gather x1, waiting for transfers between devices, on_device(): lax.all_gather(jnp.where(core == 0, query_weight, jnp.concatenate([key_we...  47.1 us
    all_to_all x1, waiting for transfers between devices, attend(): lax.all_to_all(partial.reshape(n_group, member_part, -1), 'th', 0, 0, til...  36.5 us
    dot_general x3, matrix products, tile(): jnp.einsum('qkgd,ktd->kgqt', q_chunks[chunk], k_block, preferred_element_...  22.6 us
    dot_general x3, matrix products, tile(): jnp.einsum('kgqt,ktd->qkgd', weights.astype(jnp.bfloat16), v_block, prefe...  19.8 us
    unnamed x2, matrix products  11.9 us
    slice x2, local copies, waits for them, and re-layouts, on_device(): key_rows = kv_all[0]  7.37 us
    all_gather x1, local copies, waits for them, and re-layouts, on_device(): lax.all_gather(jnp.where(core == 0, query_weight, jnp.concatenate([key_we...  6.81 us
  transfers between devices with their start and end apart: 6, of which 3 were waited for; matrix products, arithmetic and copies ran while one was open for 31% of the time, Pallas kernels for 0%

profile of v6, /device:TPU:4, one launch (start us, length us, event | category | flops | bytes accessed | tf_op | source)
XLA Modules:
  0.0 301.4 jit_solution(2232175250130506659)
XLA Ops:
  10.6 3.1 %maximum_select_fusion.1 = bf16[4608,128]{1,0:T(8,128)(2,1)} fusion(bf16[4608,128]{1,0:T(8,128)(2,1)} %param.14, bf16[4608,64]{1,0:T(8,128)(2,1)S(1)} %copy.66, bf16[4608,64]{1,0:T(8,128)(2,1)S(1)} %copy.65, pred[]{:T(512)S(6)} %eq.90), kind=kLoop, calls=%fused_computation.54 | loop fusion | flops 2949120 | bytes 3538945 | tf_op jit(solution)/shard_map/jit(_where)/select_n | solution.py:80
  14.2 2.6 broadcast_in_dim.120
  16.7 5.1 %all-to-all-start = ((bf16[8,64,4608]{2,1,0:T(8,128)(2,1)}), bf16[8,64,4608]{2,1,0:T(8,128)(2,1)}, u32[]{:S(2)}, u32[]{:S(2)}) async-start(bf16[8,64,4608]{2,1,0:T(8,128)(2,1)} %broadcast_in_dim.120), calls=%async_computation | async-start | bytes 9437184 | tf_op jit(solution)/shard_map/all_to_all | solution.py:89
  21.9 47.1 %all-gather.9.cloned.1.call-done = bf16[18432,128]{1,0:T(8,128)(2,1)} async-done(((bf16[4608,128]{1,0:T(8,128)(2,1)}), bf16[18432,128]{1,0:T(8,128)(2,1)}) %all-gather.9.cloned.1.call-update) | async-done | bytes 4718608 | tf_op jit(solution)/shard_map/all_gather | solution.py:79
  69.0 6.8 %copy.67 = bf16[4,4608,128]{1,2,0:T(8,128)(2,1)} copy(bf16[4,4608,128]{2,1,0:T(8,128)(2,1)} %bitcast.101) | data formatting | bytes 9437184 | tf_op jit(solution)/shard_map/all_gather | solution.py:79
  76.0 3.1 %gather_fusion = s32[512]{0:T(512)S(1)} fusion(s32[8192]{0:T(1024)S(1)} %copy-done, s32[1024]{0:T(1024)S(1)} %pad_clamp_fusion), kind=kCustom, calls=%fused_computation | custom fusion | bytes 6144 | tf_op jit(solution)/shard_map/jit(_take)/gather | solution.py:111
  79.9 2.6 fusion.62
  84.1 5.9 %fusion.69 = f32[512,512]{0,1:S(1)} fusion(bf16[512,4608]{1,0:T(8,128)(2,1)} %bitcast.3, bf16[4608,512]{0,1:T(8,128)(2,1)} %bitcast.100), kind=kOutput, calls=%fused_computation.135 | convolution fusion | flops 2415919104 | bytes 10485760
  90.1 5.9 %fusion.70 = f32[512,512]{0,1:S(1)} fusion(bf16[512,4608]{1,0:T(8,128)(2,1)} %bitcast.3, bf16[4608,512]{0,1:T(8,128)(2,1)} %bitcast.9), kind=kOutput, calls=%fused_computation.136 | convolution fusion | flops 2415919104 | bytes 10485760
  104.4 65.0 %all-gather.5.cloned.1.call-done = bf16[2,2,8192,128]{3,2,1,0:T(8,128)(2,1)} async-done(((bf16[2,2,512,128]{3,2,1,0:T(8,128)(2,1)}), bf16[2,2,8192,128]{3,2,1,0:T(8,128)(2,1)}) %all-gather.5.cloned.1.call-update) | async-done | bytes 8388624 | tf_op jit(solution)/shard_map/all_gather | solution.py:119
  169.4 4.4 %fusion.67 = (bf16[1,2,4,8,4,64,128]{6,5,3,4,2,1,0:T(8,128)(2,1)S(1)}, bf16[1,2,4,8,4,64,128]{6,5,3,4,2,1,0:T(8,128)(2,1)S(1)}) fusion(bf16[2,2,4,8,4,64,128]{6,5,3,4,2,1,0:T(8,128)(2,1)} %bitcast.99), kind=kLoop, calls=%fused_computation.133 | loop fusion | bytes 16777216 | tf_op jit(solution)/shard_map/slice | solution.py:122
  173.8 2.9 copy.74
  176.7 2.9 copy.75
  179.8 47.7 %while.15 = (s32[]{:T(128)}, f32[512,2,2,128]{0,3,2,1:T(8,128)S(1)}, f32[2,2,512]{2,1,0:T(2,128)S(1)}, s32[]{:T(128)}, bf16[2,8192,128]{2,1,0:T(8,128)(2,1)}, /*...) while((s32[]{:T(128)}, ...), condition=%wide.region_7.8_spmd.clone, body=%wide.region_5.7_spmd.clone.sunk | while | flops 2192845312 | bytes 41498840 | solution.py:176
  181.6 7.6 %fusion.88 = (f32[2,2,512]{2,1,0:T(2,128)S(1)}, f32[2,2048,512,2]{2,1,3,0:T(8,128)S(1)}) fusion(pred[512,2048]{0,1:T(8,128)(4,1)S(1)} %compare_and_fusion.2, bf16[512,2,2,128]{3,0,2,1:T(8,128)(2,1)S(1)} %bitcast.110, bf16[2,8192,128]{2,1,0:T(8,128)(2,1)} %get-tuple-element.383, s32[]{:T(128)S(6)} %select_n.348), kind=kOutput, calls=%fused_computation.3.clone.1 | convolution fusion | flops 1094711296 | bytes 19406852 | tf_op jit(solution)/shard_map/while/body/qkgd,ktd->kgqt/dot_general | solution.py:150
  189.2 6.6 %fusion.89 = f32[512,2,2,128]{0,3,2,1:T(8,128)S(1)} fusion(f32[512,2,2,128]{0,3,2,1:T(8,128)S(1)} %get-tuple-element.362, f32[2,2048,512,2]{2,1,3,0:T(8,128)S(1)} %get-tuple-element.344, pred[512,2048]{0,1:T(8,128)(4,1)S(1)} %compare_and_fusion.2, bf16[2,8192,128]{2,1,0:T(8,128)(2,1)} %get-tuple-element.380, s32[]{:T(128)S(6)} %select_n.348), kind=kOutput, calls=%fused_computation.9.clone.1 | convolution fusion | flops 1094975488 | bytes 20971524 | tf_op jit(solution)/shard_map/while/body/kgqt,ktd->qkgd/dot_general | solution.py:164
  197.5 7.5 %fusion.88 = (f32[2,2,512]{2,1,0:T(2,128)S(1)}, f32[2,2048,512,2]{2,1,3,0:T(8,128)S(1)}) fusion(pred[512,2048]{0,1:T(8,128)(4,1)S(1)} %compare_and_fusion.2, bf16[512,2,2,128]{3,0,2,1:T(8,128)(2,1)S(1)} %bitcast.110, bf16[2,8192,128]{2,1,0:T(8,128)(2,1)} %get-tuple-element.383, s32[]{:T(128)S(6)} %select_n.348), kind=kOutput, calls=%fused_computation.3.clone.1 | convolution fusion | flops 1094711296 | bytes 19406852 | tf_op jit(solution)/shard_map/while/body/qkgd,ktd->kgqt/dot_general | solution.py:150
  205.0 6.6 %fusion.89 = f32[512,2,2,128]{0,3,2,1:T(8,128)S(1)} fusion(f32[512,2,2,128]{0,3,2,1:T(8,128)S(1)} %get-tuple-element.362, f32[2,2048,512,2]{2,1,3,0:T(8,128)S(1)} %get-tuple-element.344, pred[512,2048]{0,1:T(8,128)(4,1)S(1)} %compare_and_fusion.2, bf16[2,8192,128]{2,1,0:T(8,128)(2,1)} %get-tuple-element.380, s32[]{:T(128)S(6)} %select_n.348), kind=kOutput, calls=%fused_computation.9.clone.1 | convolution fusion | flops 1094975488 | bytes 20971524 | tf_op jit(solution)/shard_map/while/body/kgqt,ktd->qkgd/dot_general | solution.py:164
  213.3 7.5 %fusion.88 = (f32[2,2,512]{2,1,0:T(2,128)S(1)}, f32[2,2048,512,2]{2,1,3,0:T(8,128)S(1)}) fusion(pred[512,2048]{0,1:T(8,128)(4,1)S(1)} %compare_and_fusion.2, bf16[512,2,2,128]{3,0,2,1:T(8,128)(2,1)S(1)} %bitcast.110, bf16[2,8192,128]{2,1,0:T(8,128)(2,1)} %get-tuple-element.383, s32[]{:T(128)S(6)} %select_n.348), kind=kOutput, calls=%fused_computation.3.clone.1 | convolution fusion | flops 1094711296 | bytes 19406852 | tf_op jit(solution)/shard_map/while/body/qkgd,ktd->kgqt/dot_general | solution.py:150
  220.8 6.6 %fusion.89 = f32[512,2,2,128]{0,3,2,1:T(8,128)S(1)} fusion(f32[512,2,2,128]{0,3,2,1:T(8,128)S(1)} %get-tuple-element.362, f32[2,2048,512,2]{2,1,3,0:T(8,128)S(1)} %get-tuple-element.344, pred[512,2048]{0,1:T(8,128)(4,1)S(1)} %compare_and_fusion.2, bf16[2,8192,128]{2,1,0:T(8,128)(2,1)} %get-tuple-element.380, s32[]{:T(128)S(6)} %select_n.348), kind=kOutput, calls=%fused_computation.9.clone.1 | convolution fusion | flops 1094975488 | bytes 20971524 | tf_op jit(solution)/shard_map/while/body/kgqt,ktd->qkgd/dot_general | solution.py:164
  227.7 6.6 %convolution_convert_fusion = bf16[512,4608]{1,0:T(8,128)(2,1)} fusion(bf16[512,512]{0,1:T(8,128)(2,1)S(1)} %bitcast.104, bf16[512,4608]{1,0:T(8,128)(2,1)} %all-gather.7.cloned.1.call-done), kind=kOutput, calls=%fused_computation.39 | convolution fusion | flops 2418278400 | bytes 9961472 | tf_op jit(solution)/shard_map/dot_general | solution.py:181
  234.2 5.8 %all-to-all-start.1 = ((bf16[8,64,4608]{2,1,0:T(8,128)(2,1)}), bf16[8,64,4608]{2,1,0:T(8,128)(2,1)}, u32[]{:S(2)}, u32[]{:S(2)}) async-start(bf16[8,64,4608]{2,1,0:T(8,128)(2,1)} %bitcast.96), calls=%async_computation.1 | async-start | bytes 9437184 | tf_op jit(solution)/shard_map/all_to_all | solution.py:184
  253.9 36.5 %all-to-all-done.1 = bf16[8,64,4608]{2,1,0:T(8,128)(2,1)} async-done(((bf16[8,64,4608]{2,1,0:T(8,128)(2,1)}), bf16[8,64,4608]{2,1,0:T(8,128)(2,1)}, u32[]{:S(2)}, u32[]{:S(2)}) %all-to-all-start.1) | async-done | bytes 4718624 | tf_op jit(solution)/shard_map/all_to_all | solution.py:184
  290.5 3.1 %convert_reduce_fusion = f32[64,4608]{1,0:T(8,128)S(1)} fusion(bf16[8,64,4608]{2,1,0:T(8,128)(2,1)} %all-to-all-done.1), kind=kLoop, calls=%fused_computation.38 | loop fusion | flops 4423680 | bytes 5898240 | tf_op jit(solution)/shard_map/reduce_sum | solution.py:187
  (81 shorter events, 28.0 us)
Async XLA Ops:
  7.2 61.8 %all-gather.9.cloned.1.call-start = ((), (), s32[]{:S(2)}) async-start(), calls=%async_computation.4 | async-start | bytes 5898240 | tf_op jit(solution)/shard_map/all_gather | solution.py:79
  8.9 4.8 %copy-start.1 = (bf16[64,4608]{1,0:T(8,128)(2,1)S(1)}, bf16[64,4608]{1,0:T(8,128)(2,1)}, u32[]{:S(2)}) copy-start(bf16[64,4608]{1,0:T(8,128)(2,1)} %param.12) | copy-start | bytes 1769476
  8.9 5.1 %copy-start.3 = (f32[4608]{0:T(1024)S(1)}, f32[4608]{0:T(1024)}, u32[]{:S(2)}) copy-start(f32[4608]{0:T(1024)} %param.13) | copy-start | bytes 55300
  16.7 67.4 %all-to-all-start = ((bf16[8,64,4608]{2,1,0:T(8,128)(2,1)}), bf16[8,64,4608]{2,1,0:T(8,128)(2,1)}, u32[]{:S(2)}, u32[]{:S(2)}) async-start(bf16[8,64,4608]{2,1,0:T(8,128)(2,1)} %broadcast_in_dim.120), calls=%async_computation | async-start | bytes 9437184 | tf_op jit(solution)/shard_map/all_to_all | solution.py:89
  21.8 147.6 %all-gather.5.cloned.1.call-start = ((), (), s32[]{:S(2)}) async-start(), calls=%async_computation.2 | async-start | bytes 8912896 | tf_op jit(solution)/shard_map/all_gather | solution.py:119
  69.0 6.8 %copy-start.5 = (s32[3]{0:T(128)S(1)}, s32[3]{0:T(128)}, u32[]{:S(2)}) copy-start(s32[3]{0:T(128)} %param.19) | copy-start | bytes 40
  69.0 7.0 %copy-start = (s32[8192]{0:T(1024)S(1)}, s32[8192]{0:T(1024)}, u32[]{:S(2)}) copy-start(s32[8192]{0:T(1024)} %param.20) | copy-start | bytes 98308
  69.0 10.2 %copy-start.6 = (s32[3]{0:T(128)S(1)}, s32[3]{0:T(128)}, u32[]{:S(2)}) copy-start(s32[3]{0:T(128)} %param.21) | copy-start | bytes 40
  75.8 14.3 %collective-permute-start = (bf16[4,4608,128]{1,2,0:T(8,128)(2,1)}, bf16[4,4608,128]{1,2,0:T(8,128)(2,1)}, u32[]{:S(2)}, u32[]{:S(2)}) collective-permute-start(bf16[4,4608,128]{1,2,0:T(8,128)(2,1)} %copy.67), channel_id=1, source_target_pairs={{0,32},{32,0},{64,96},{96,64},{1,33},{33,1},{65,97},{97,65},{2,34}... | collective-permute-start | bytes 14155784 | tf_op jit(solution)/shard_map/ppermute | solution.py:85
  98.4 129.3 %all-gather.7.cloned.1.call-start = ((), (), s32[]{:S(2)}) async-start(), calls=%async_computation.3 | async-start | bytes 5898240 | tf_op jit(solution)/shard_map/all_gather | solution.py:86
  234.2 56.2 %all-to-all-start.1 = ((bf16[8,64,4608]{2,1,0:T(8,128)(2,1)}), bf16[8,64,4608]{2,1,0:T(8,128)(2,1)}, u32[]{:S(2)}, u32[]{:S(2)}) async-start(bf16[8,64,4608]{2,1,0:T(8,128)(2,1)} %bitcast.96), calls=%async_computation.1 | async-start | bytes 9437184 | tf_op jit(solution)/shard_map/all_to_all | solution.py:184
  252.3 41.5 %copy-start.2 = (bf16[64,4608]{1,0:T(8,128)(2,1)S(1)}, bf16[64,4608]{1,0:T(8,128)(2,1)}, u32[]{:S(2)}) copy-start(bf16[64,4608]{1,0:T(8,128)(2,1)} %param.12) | copy-start | bytes 1769476
  252.3 41.5 %copy-start.4 = (f32[4608]{0:T(1024)S(1)}, f32[4608]{0:T(1024)}, u32[]{:S(2)}) copy-start(f32[4608]{0:T(1024)} %param.18) | copy-start | bytes 55300
Sparse Core Ops, SparseCore 0:
  13.8 55.1 all-gather.8
  98.5 70.8 all-gather.4
  171.0 52.8 all-gather.6
